TPU v7x, 256 devices: a whole 4x4x8 slice. The times are simulated.
256 devices in a mesh: dp: 8 (over y, x_hi), shard: 32 (over x_lo, z, core).
Axes of the slice: x: 4 (x_hi: 2, x_lo: 2; x = x_hi * 2 + x_lo), y: 4, z: 8, core: 2. Of those that a mesh axis runs over, the one named last changes fastest.
Arguments:
- grads: float32 [8, 1, 2, 4096, 4096], P('dp', None, None, None, 'shard'), may hold values from -6 to 6
- params: float32 [1, 2, 4096, 4096], P(None, None, ('dp', 'shard')), may hold values from -0.09375 to 0.09375
- moment_one: float32 [1, 2, 4096, 4096], P(None, None, ('dp', 'shard')), may hold values from -0.75 to 0.75
- moment_two: float32 [1, 2, 4096, 4096], P(None, None, ('dp', 'shard')), may hold values from 1e-05 to 0.01
- relation_ids: int32 [1], replicated, may hold values from 0 to 63
- rates: float32 [64], replicated, may hold values from 0.02 to 0.1
- step_count: int32 [1], replicated, may hold values from 1 to 8
Outputs:
- new_params: float32 [1, 2, 4096, 4096], P(None, None, ('dp', 'shard'))
- new_moment_one: float32 [1, 2, 4096, 4096], P(None, None, ('dp', 'shard'))
- new_moment_two: float32 [1, 2, 4096, 4096], P(None, None, ('dp', 'shard'))
- panels: bfloat16 [1, 2, 4096, 4096], P(None, None, None, 'shard')
Inputs may be any that keep to these rules, and one draw needn't show every extreme that they name: `relation_ids`: relation ids are edge types. `step_count`: the step count is positive.
All inputs are finite; a program needn't handle non-finite values.
Results may differ from a plain program's by a relative error of at most 0.001.
Values may be sent and summed in bfloat16 or wider, within the bound.
No kernel may reach another device: no remote copies, remote signals or barrier semaphores. Data moves between devices by JAX's collectives and lax.ppermute only.
A program may use at most 128 MiB of HBM per device.

v0:
```python
import jax
import jax.numpy as jnp
from jax import lax
from jax.sharding import PartitionSpec as P


def _dp_rings(groups):
    ring = groups // 2
    plus = [(2 * y + h, 2 * ((y + 1) % ring) + h) for y in range(ring) for h in range(2)]
    minus = [(2 * y + h, 2 * ((y - 1) % ring) + h) for y in range(ring) for h in range(2)]
    partner = [(2 * y + h, 2 * y + 1 - h) for y in range(ring) for h in range(2)]
    return ring, plus, minus, partner


def _take(x, index):
    return lax.dynamic_index_in_dim(x, index, axis=1, keepdims=False)


def _reduce_scatter_dp(x, groups):
    ring, plus, minus, partner = _dp_rings(groups)
    d = lax.axis_index("dp")
    y = d // 2
    h = d % 2
    up = _take(x, 2 * ((y - 1) % ring))
    down = _take(x, 2 * ((y + 1) % ring) + 1)
    for t in range(ring - 1):
        up = lax.ppermute(up, "dp", plus)
        down = lax.ppermute(down, "dp", minus)
        up = up + _take(x, 2 * ((y - t - 2) % ring))
        down = down + _take(x, 2 * ((y + t + 2) % ring) + 1)
    keep = lax.select(h == 0, up, down)
    send = lax.select(h == 0, down, up)
    return keep + lax.ppermute(send, "dp", partner)


def _all_gather_dp(mine, groups):
    ring, plus, minus, partner = _dp_rings(groups)
    d = lax.axis_index("dp")
    y = d // 2
    h = d % 2
    other = lax.ppermute(mine, "dp", partner)
    even = lax.select(h == 0, mine, other)
    odd = lax.select(h == 0, other, mine)
    lead, block, cols = mine.shape
    out = jnp.zeros((lead, ring, 2, block, cols), mine.dtype)
    out = lax.dynamic_update_slice(out, jnp.stack([even, odd], axis=1)[:, None], (0, y, 0, 0, 0))
    up, down = even, odd
    for t in range(ring - 1):
        up = lax.ppermute(up, "dp", plus)
        down = lax.ppermute(down, "dp", minus)
        out = lax.dynamic_update_slice(out, up[:, None, None], (0, (y - t - 1) % ring, 0, 0, 0))
        out = lax.dynamic_update_slice(out, down[:, None, None], (0, (y + t + 1) % ring, 1, 0, 0))
    return out.reshape(lead, groups * block, cols)


def _adam(gradient, params, moment_one, moment_two, learn, fix_one, fix_two):
    new_one = 0.9 * moment_one + 0.1 * gradient
    new_two = 0.95 * moment_two + 0.05 * gradient * gradient
    update = new_one / fix_one / (jnp.sqrt(new_two / fix_two) + 1e-08) + 0.1 * params
    return params - learn * update, new_one, new_two


def _step(grads, params, moment_one, moment_two, relation_ids, rates, step_count):
    groups = lax.axis_size("dp")
    owners = lax.axis_size("shard")
    relations = grads.shape[1]
    rows = grads.shape[3]
    panel_cols = grads.shape[-1]
    owned = params.shape[2]
    block = rows // groups
    lead = relations * 2
    onehot = (relation_ids[:, None] == jnp.arange(rates.shape[0], dtype=jnp.int32)[None, :]).astype(
        jnp.float32
    )
    learn = jnp.sum(onehot * rates[None, :], axis=1)[:, None, None, None]
    steps = step_count[0].astype(jnp.float32)
    fix_one = 1.0 - jnp.power(jnp.float32(0.9), steps)
    fix_two = 1.0 - jnp.power(jnp.float32(0.95), steps)
    state = jnp.stack([params, moment_one, moment_two]).reshape(3, relations, 2, 1, owned, owners, panel_cols)
    state = lax.all_to_all(state, "shard", split_axis=5, concat_axis=3, tiled=True)
    state = state.reshape(3, relations, 2, block, panel_cols)
    local = grads.reshape(lead, groups, block, panel_cols)
    ringed = block * 5 // 8
    offload = lax.psum_scatter(local[:, :, ringed:].reshape(lead, -1, panel_cols), "dp", scatter_dimension=1, tiled=True)
    summed = _reduce_scatter_dp(local[:, :, :ringed], groups)
    summed = jnp.concatenate([summed, offload], axis=1)
    gradient = summed.reshape(relations, 2, block, panel_cols) / groups
    fresh, _, _ = _adam(gradient, state[0], state[1], state[2], learn, fix_one, fix_two)
    fresh = fresh.astype(jnp.bfloat16).reshape(lead, block, panel_cols)
    panels = _all_gather_dp(fresh, groups).reshape(relations, 2, rows, panel_cols)
    moved = (summed / groups).reshape(relations, 2, owners, owned, 1, panel_cols)
    moved = lax.all_to_all(moved, "shard", split_axis=2, concat_axis=4, tiled=True)
    moved = moved.reshape(relations, 2, owned, owners * panel_cols)
    new_params, new_one, new_two = _adam(moved, params, moment_one, moment_two, learn, fix_one, fix_two)
    return (new_params, new_one, new_two, panels)


def solution(mesh):
    in_specs = (
        P("dp", None, None, None, "shard"),
        P(None, None, ("dp", "shard"), None),
        P(None, None, ("dp", "shard"), None),
        P(None, None, ("dp", "shard"), None),
        P(),
        P(),
        P(),
    )
    out_specs = (
        P(None, None, ("dp", "shard"), None),
        P(None, None, ("dp", "shard"), None),
        P(None, None, ("dp", "shard"), None),
        P(None, None, None, "shard"),
    )
    return jax.shard_map(_step, mesh=mesh, in_specs=in_specs, out_specs=out_specs, check_vma=False)
```

profile of v0, /device:TPU:32, one launch (start us, length us, event | category | flops | bytes accessed | tf_op | source)
XLA Modules:
  0.0 163.4 jit_solution(10628029523410615943)
XLA Ops:
  9.8 2.1 %copy.48 = f32[3,1,2,1,16,32,128]{6,4,2,3,1,0,5:T(8,128)} copy(f32[3,1,2,1,16,32,128]{6,5,0,4,2,3,1:T(8,128)S(1)} %pad_maximum_fusion) | data formatting | bytes 3145728 | tf_op jit(solution)/shard_map/stack | solution.py:79
  11.9 9.7 %all-to-all-start.1 = ((f32[3,1,2,1,16,32,128]{6,4,2,3,1,0,5:T(8,128)}), f32[3,1,2,1,16,32,128]{6,4,2,3,1,0,5:T(8,128)}, u32[]{:S(2)}, u32[]{:S(2)}) async-start(f32[3,1,2,1,16,32,128]{6,4,2,3,1,0,5:T(8,128)} %copy.48), calls=%async_computation.2 | async-start | bytes 3145728 | tf_op jit(solution)/shard_map/all_to_all | solution.py:80
  21.6 2.7 %slice.24 = f32[2,8,192,128]{3,2,1,0:T(8,128)} slice(f32[2,8,512,128]{3,2,1,0:T(8,128)} %bitcast.85), slice={[0:2], [0:8], [320:512], [0:128]} | slice | bytes 3145728 | tf_op jit(solution)/shard_map/slice | solution.py:84
  24.4 1.9 %slice.23 = f32[2,8,320,128]{3,2,1,0:T(8,128)S(1)} slice(f32[2,8,512,128]{3,2,1,0:T(8,128)} %bitcast.86), slice={[0:2], [0:8], [0:320], [0:128]} | slice | bytes 5242880 | tf_op jit(solution)/shard_map/slice | solution.py:85
  30.4 8.0 %collective-permute-done = f32[2,320,128]{2,1,0:T(8,128)S(1)} collective-permute-done((f32[2,320,128]{2,1,0:T(8,128)}, f32[2,320,128]{2,1,0:T(8,128)S(1)}, u32[]{:S(2)}, u32[]{:S(2)}) %collective-permute-start) | collective-permute-done | bytes 327712 | tf_op jit(solution)/shard_map/ppermute | solution.py:27
  38.4 1.8 %bitcast_add_fusion.2 = (f32[2,320,128]{2,1,0:T(8,128)S(1)}, f32[2,320,128]{2,1,0:T(8,128)}) fusion(f32[2,320,128]{2,1,0:T(8,128)} %collective-permute-done.3, f32[2,8,320,128]{3,2,1,0:T(8,128)S(1)} %slice.23, s32[]{:T(128)S(6)} %select_n.138, f32[2,320,128]{2,1,0:T(8,128)S(1)} %collective-permute-done, s32[]{:T(128)S(6)} %select_n.130), kind=kLoop, calls=%fused_computation.15 | loop fusion | flops 163840 | bytes 1966088 | tf_op jit(solution)/shard_map/add | solution.py:30
  41.6 1.7 %collective-permute-start.4 = (f32[2,320,128]{2,1,0:T(8,128)S(1)}, f32[2,320,128]{2,1,0:T(8,128)}, u32[]{:S(2)}, u32[]{:S(2)}) collective-permute-start(f32[2,320,128]{2,1,0:T(8,128)S(1)} %get-tuple-element.13), channel_id=1, source_target_pairs={{0,192},{32,224},{64,0},{96,32},{128,64},{160,96},{192,128},{224,1... | collective-permute-start | bytes 983048 | tf_op jit(solution)/shard_map/ppermute | solution.py:28
  43.4 9.1 %collective-permute-done.1 = f32[2,320,128]{2,1,0:T(8,128)S(1)} collective-permute-done((f32[2,320,128]{2,1,0:T(8,128)}, f32[2,320,128]{2,1,0:T(8,128)S(1)}, u32[]{:S(2)}, u32[]{:S(2)}) %collective-permute-start.1) | collective-permute-done | bytes 327712 | tf_op jit(solution)/shard_map/ppermute | solution.py:27
  52.4 1.9 %bitcast_add_fusion.1 = (f32[2,320,128]{2,1,0:T(8,128)}, f32[2,320,128]{2,1,0:T(8,128)}) fusion(f32[2,320,128]{2,1,0:T(8,128)} %collective-permute-done.4, f32[2,8,320,128]{3,2,1,0:T(8,128)S(1)} %slice.23, s32[]{:T(128)S(6)} %select_n.140, f32[2,320,128]{2,1,0:T(8,128)S(1)} %collective-permute-done.1, s32[]{:T(128)S(6)} %select_n.132), kind=kLoop, calls=%fused_computation.14 | loop fusion | flops 163840 | bytes 1966088 | tf_op jit(solution)/shard_map/add | solution.py:30
  55.1 2.5 %collective-permute-start.5 = (f32[2,320,128]{2,1,0:T(8,128)}, f32[2,320,128]{2,1,0:T(8,128)S(1)}, u32[]{:S(2)}, u32[]{:S(2)}) collective-permute-start(f32[2,320,128]{2,1,0:T(8,128)} %get-tuple-element.11), channel_id=1, source_target_pairs={{0,192},{32,224},{64,0},{96,32},{128,64},{160,96},{192,128},{224,1... | collective-permute-start | bytes 983048 | tf_op jit(solution)/shard_map/ppermute | solution.py:28
  57.6 8.2 %collective-permute-done.2 = f32[2,320,128]{2,1,0:T(8,128)S(1)} collective-permute-done((f32[2,320,128]{2,1,0:T(8,128)}, f32[2,320,128]{2,1,0:T(8,128)S(1)}, u32[]{:S(2)}, u32[]{:S(2)}) %collective-permute-start.2) | collective-permute-done | bytes 327712 | tf_op jit(solution)/shard_map/ppermute | solution.py:27
  65.9 3.1 %collective-permute-start.6 = (f32[2,320,128]{2,1,0:T(8,128)S(1)}, f32[2,320,128]{2,1,0:T(8,128)S(1)}, u32[]{:S(2)}, u32[]{:S(2)}) collective-permute-start(f32[2,320,128]{2,1,0:T(8,128)S(1)} %broadcast_select_fusion.2), channel_id=1, source_target_pairs={{0,32},{32,0},{64,96},{96,64},{128,160},{160,128},{192,224},{224,1... | collective-permute-start | bytes 983048 | tf_op jit(solution)/shard_map/ppermute | solution.py:33
  71.0 5.7 %collective-permute-done.6 = f32[2,320,128]{2,1,0:T(8,128)S(1)} collective-permute-done((f32[2,320,128]{2,1,0:T(8,128)S(1)}, f32[2,320,128]{2,1,0:T(8,128)S(1)}, u32[]{:S(2)}, u32[]{:S(2)}) %collective-permute-start.6) | collective-permute-done | bytes 327712 | tf_op jit(solution)/shard_map/ppermute | solution.py:33
  79.5 29.6 %reduce-scatter.2.cloned.1.call-done = f32[2,192,128]{2,1,0:T(8,128)} async-done(((f32[2,1536,128]{2,1,0:T(8,128)}), f32[2,192,128]{2,1,0:T(8,128)}) %reduce-scatter.2.cloned.1.call-update) | async-done | bytes 196624 | tf_op jit(solution)/shard_map/reduce_scatter | solution.py:84
  109.1 1.9 %subtract_convert_fusion = (bf16[2,512,128]{2,1,0:T(8,128)(2,1)S(1)}, f32[2,512,128]{2,1,0:T(8,128)S(1)}) fusion(f32[2,512,128]{2,1,0:T(8,128)S(1)} %bitcast.98, f32[2,512,128]{2,1,0:T(8,128)S(1)} %bitcast.97, f32[2,512,128]{2,1,0:T(8,128)S(1)} %bitcast.96, f32[2,192,128]{2,1,0:T(8,128)} %reduce-scatter.2.cloned.1.call-done, ...), kind=kLoop, calls=%fused_computation.9 | loop fusion | flops 2097152 | bytes 2883596 | tf_op jit(solution)/shard_map/convert_element_type | solution.py:89
  111.0 2.1 %collective-permute-start.7 = (bf16[2,512,128]{2,1,0:T(8,128)(2,1)S(1)}, bf16[2,512,128]{2,1,0:T(8,128)(2,1)S(1)}, u32[]{:S(2)}, u32[]{:S(2)}) collective-permute-start(bf16[2,512,128]{2,1,0:T(8,128)(2,1)S(1)} %get-tuple-element.22), channel_id=1, source_target_pairs={{0,32},{32,0},{64,96},{96,64},{128,160},{160,128},{192,224},{224,1... | collective-permute-start | bytes 786440 | tf_op jit(solution)/shard_map/ppermute | solution.py:41
  113.2 5.8 %collective-permute-done.7 = bf16[2,512,128]{2,1,0:T(8,128)(2,1)S(1)} collective-permute-done((bf16[2,512,128]{2,1,0:T(8,128)(2,1)S(1)}, bf16[2,512,128]{2,1,0:T(8,128)(2,1)S(1)}, u32[]{:S(2)}, u32[]{:S(2)}) %collective-permute-start.7) | collective-permute-done | bytes 262176 | tf_op jit(solution)/shard_map/ppermute | solution.py:41
  120.8 2.1 %collective-permute-start.9 = (bf16[2,512,128]{2,1,0:T(8,128)(2,1)S(1)}, bf16[2,512,128]{2,1,0:T(8,128)(2,1)}, u32[]{:S(2)}, u32[]{:S(2)}) collective-permute-start(bf16[2,512,128]{2,1,0:T(8,128)(2,1)S(1)} %get-tuple-element.21), channel_id=1, source_target_pairs={{0,192},{32,224},{64,0},{96,32},{128,64},{160,96},{192,128},{224,1... | collective-permute-start | bytes 786440 | tf_op jit(solution)/shard_map/ppermute | solution.py:50
  123.8 7.7 %all-to-all-start = ((f32[1,2,32,16,1,128]{5,3,1,4,0,2:T(8,128)}), f32[1,2,32,16,1,128]{5,3,1,4,0,2:T(8,128)S(1)}, u32[]{:S(2)}, u32[]{:S(2)}) async-start(f32[1,2,32,16,1,128]{5,3,1,4,0,2:T(8,128)} %copy.43), calls=%async_computation.1 | async-start | bytes 1048576 | tf_op jit(solution)/shard_map/all_to_all | solution.py:92
  133.3 3.2 %collective-permute-start.11 = (bf16[2,512,128]{2,1,0:T(8,128)(2,1)}, bf16[2,512,128]{2,1,0:T(8,128)(2,1)S(1)}, u32[]{:S(2)}, u32[]{:S(2)}) collective-permute-start(bf16[2,512,128]{2,1,0:T(8,128)(2,1)} %collective-permute-done.9), channel_id=1, source_target_pairs={{0,192},{32,224},{64,0},{96,32},{128,64},{160,96},{192,128},{224,1... | collective-permute-start | bytes 786440 | tf_op jit(solution)/shard_map/ppermute | solution.py:50
  138.5 4.6 %collective-permute-done.10 = bf16[2,512,128]{2,1,0:T(8,128)(2,1)} collective-permute-done((bf16[2,512,128]{2,1,0:T(8,128)(2,1)}, bf16[2,512,128]{2,1,0:T(8,128)(2,1)}, u32[]{:S(2)}, u32[]{:S(2)}) %collective-permute-start.10) | collective-permute-done | bytes 262176 | tf_op jit(solution)/shard_map/ppermute | solution.py:49
  143.2 3.2 %collective-permute-start.13 = (bf16[2,512,128]{2,1,0:T(8,128)(2,1)S(1)}, bf16[2,512,128]{2,1,0:T(8,128)(2,1)}, u32[]{:S(2)}, u32[]{:S(2)}) collective-permute-start(bf16[2,512,128]{2,1,0:T(8,128)(2,1)S(1)} %collective-permute-done.11), channel_id=1, source_target_pairs={{0,192},{32,224},{64,0},{96,32},{128,64},{160,96},{192,128},{224,1... | collective-permute-start | bytes 786440 | tf_op jit(solution)/shard_map/ppermute | solution.py:50
  147.4 1.8 %all-to-all-done = f32[1,2,32,16,1,128]{5,3,1,4,0,2:T(8,128)S(1)} async-done(((f32[1,2,32,16,1,128]{5,3,1,4,0,2:T(8,128)}), f32[1,2,32,16,1,128]{5,3,1,4,0,2:T(8,128)S(1)}, u32[]{:S(2)}, u32[]{:S(2)}) %all-to-all-start) | async-done | bytes 524320 | tf_op jit(solution)/shard_map/all_to_all | solution.py:92
  149.6 3.5 %multiply_subtract_fusion = (f32[1,2,16,4096]{3,2,1,0:T(8,128)}, f32[1,2,16,4096]{3,2,1,0:T(8,128)}, f32[1,2,16,4096]{3,2,1,0:T(8,128)}) fusion(f32[1,2,16,4096]{3,2,1,0:T(8,128)S(1)} %copy-done.1, f32[]{:T(128)} %bitcast.16, f32[]{:T(128)} %bitcast.15, f32[]{:T(128)} %fusion.3, f32[1,2,16,4096]{3,0,2,1:T(1,128)S(1)} %bitcast.92, ...), kind=kLoop, calls=%fused_computation.10 | loop fusion | flops 1966080 | bytes 3670028 | tf_op jit(solution)/shard_map/sub | solution.py:60
  (50 shorter events, 23.6 us)
Async XLA Ops:
  7.2 2.4 %copy-start.2 = (f32[1,2,16,4096]{3,2,1,0:T(8,128)S(1)}, f32[1,2,16,4096]{3,2,1,0:T(8,128)}, u32[]{:S(2)}) copy-start(f32[1,2,16,4096]{3,2,1,0:T(8,128)} %param.10) | copy-start | bytes 1572868
  11.9 65.9 %all-to-all-start.1 = ((f32[3,1,2,1,16,32,128]{6,4,2,3,1,0,5:T(8,128)}), f32[3,1,2,1,16,32,128]{6,4,2,3,1,0,5:T(8,128)}, u32[]{:S(2)}, u32[]{:S(2)}) async-start(f32[3,1,2,1,16,32,128]{6,4,2,3,1,0,5:T(8,128)} %copy.48), calls=%async_computation.2 | async-start | bytes 3145728 | tf_op jit(solution)/shard_map/all_to_all | solution.py:80
  21.6 87.6 %reduce-scatter.2.cloned.1.call-start = ((), (), s32[]{:S(2)}) async-start(), calls=%async_computation.3 | async-start | bytes 1769472 | tf_op jit(solution)/shard_map/reduce_scatter | solution.py:84
  27.1 11.2 %collective-permute-start = (f32[2,320,128]{2,1,0:T(8,128)}, f32[2,320,128]{2,1,0:T(8,128)S(1)}, u32[]{:S(2)}, u32[]{:S(2)}) collective-permute-start(f32[2,320,128]{2,1,0:T(8,128)} %get-tuple-element.16), channel_id=1, source_target_pairs={{0,64},{32,96},{64,128},{96,160},{128,192},{160,224},{192,0},{224,... | collective-permute-start | bytes 983048 | tf_op jit(solution)/shard_map/ppermute | solution.py:27
  28.7 9.6 %collective-permute-start.3 = (f32[2,320,128]{2,1,0:T(8,128)S(1)}, f32[2,320,128]{2,1,0:T(8,128)}, u32[]{:S(2)}, u32[]{:S(2)}) collective-permute-start(f32[2,320,128]{2,1,0:T(8,128)S(1)} %get-tuple-element.15), channel_id=1, source_target_pairs={{0,192},{32,224},{64,0},{96,32},{128,64},{160,96},{192,128},{224,1... | collective-permute-start | bytes 983048 | tf_op jit(solution)/shard_map/ppermute | solution.py:28
  40.1 30.3 %copy-start.4 = (f32[64]{0:T(128)S(1)}, f32[64]{0:T(128)}, u32[]{:S(2)}) copy-start(f32[64]{0:T(128)} %param.12) | copy-start | bytes 772
  40.1 12.3 %collective-permute-start.1 = (f32[2,320,128]{2,1,0:T(8,128)}, f32[2,320,128]{2,1,0:T(8,128)S(1)}, u32[]{:S(2)}, u32[]{:S(2)}) collective-permute-start(f32[2,320,128]{2,1,0:T(8,128)} %get-tuple-element.14), channel_id=1, source_target_pairs={{0,64},{32,96},{64,128},{96,160},{128,192},{160,224},{192,0},{224,... | collective-permute-start | bytes 983048 | tf_op jit(solution)/shard_map/ppermute | solution.py:27
  41.6 10.8 %collective-permute-start.4 = (f32[2,320,128]{2,1,0:T(8,128)S(1)}, f32[2,320,128]{2,1,0:T(8,128)}, u32[]{:S(2)}, u32[]{:S(2)}) collective-permute-start(f32[2,320,128]{2,1,0:T(8,128)S(1)} %get-tuple-element.13), channel_id=1, source_target_pairs={{0,192},{32,224},{64,0},{96,32},{128,64},{160,96},{192,128},{224,1... | collective-permute-start | bytes 983048 | tf_op jit(solution)/shard_map/ppermute | solution.py:28
  54.3 11.5 %collective-permute-start.2 = (f32[2,320,128]{2,1,0:T(8,128)}, f32[2,320,128]{2,1,0:T(8,128)S(1)}, u32[]{:S(2)}, u32[]{:S(2)}) collective-permute-start(f32[2,320,128]{2,1,0:T(8,128)} %get-tuple-element.12), channel_id=1, source_target_pairs={{0,64},{32,96},{64,128},{96,160},{128,192},{160,224},{192,0},{224,... | collective-permute-start | bytes 983048 | tf_op jit(solution)/shard_map/ppermute | solution.py:27
  55.1 10.7 %collective-permute-start.5 = (f32[2,320,128]{2,1,0:T(8,128)}, f32[2,320,128]{2,1,0:T(8,128)S(1)}, u32[]{:S(2)}, u32[]{:S(2)}) collective-permute-start(f32[2,320,128]{2,1,0:T(8,128)} %get-tuple-element.11), channel_id=1, source_target_pairs={{0,192},{32,224},{64,0},{96,32},{128,64},{160,96},{192,128},{224,1... | collective-permute-start | bytes 983048 | tf_op jit(solution)/shard_map/ppermute | solution.py:28
  65.8 5.2 %copy-start.3 = (f32[2,320,128]{2,1,0:T(8,128)}, f32[2,320,128]{2,1,0:T(8,128)S(1)}, u32[]{:S(2)}) copy-start(f32[2,320,128]{2,1,0:T(8,128)S(1)} %collective-permute-done.5) | copy-start | bytes 983044
  65.9 10.8 %collective-permute-start.6 = (f32[2,320,128]{2,1,0:T(8,128)S(1)}, f32[2,320,128]{2,1,0:T(8,128)S(1)}, u32[]{:S(2)}, u32[]{:S(2)}) collective-permute-start(f32[2,320,128]{2,1,0:T(8,128)S(1)} %broadcast_select_fusion.2), channel_id=1, source_target_pairs={{0,32},{32,0},{64,96},{96,64},{128,160},{160,128},{192,224},{224,1... | collective-permute-start | bytes 983048 | tf_op jit(solution)/shard_map/ppermute | solution.py:33
  111.0 8.0 %collective-permute-start.7 = (bf16[2,512,128]{2,1,0:T(8,128)(2,1)S(1)}, bf16[2,512,128]{2,1,0:T(8,128)(2,1)S(1)}, u32[]{:S(2)}, u32[]{:S(2)}) collective-permute-start(bf16[2,512,128]{2,1,0:T(8,128)(2,1)S(1)} %get-tuple-element.22), channel_id=1, source_target_pairs={{0,32},{32,0},{64,96},{96,64},{128,160},{160,128},{192,224},{224,1... | collective-permute-start | bytes 786440 | tf_op jit(solution)/shard_map/ppermute | solution.py:41
  119.7 13.3 %collective-permute-start.8 = (bf16[2,512,128]{2,1,0:T(8,128)(2,1)}, bf16[2,512,128]{2,1,0:T(8,128)(2,1)}, u32[]{:S(2)}, u32[]{:S(2)}) collective-permute-start(bf16[2,512,128]{2,1,0:T(8,128)(2,1)} %get-tuple-element.20), channel_id=1, source_target_pairs={{0,64},{32,96},{64,128},{96,160},{128,192},{160,224},{192,0},{224,... | collective-permute-start | bytes 786440 | tf_op jit(solution)/shard_map/ppermute | solution.py:49
  120.8 12.5 %collective-permute-start.9 = (bf16[2,512,128]{2,1,0:T(8,128)(2,1)S(1)}, bf16[2,512,128]{2,1,0:T(8,128)(2,1)}, u32[]{:S(2)}, u32[]{:S(2)}) collective-permute-start(bf16[2,512,128]{2,1,0:T(8,128)(2,1)S(1)} %get-tuple-element.21), channel_id=1, source_target_pairs={{0,192},{32,224},{64,0},{96,32},{128,64},{160,96},{192,128},{224,1... | collective-permute-start | bytes 786440 | tf_op jit(solution)/shard_map/ppermute | solution.py:50
  123.8 25.4 %all-to-all-start = ((f32[1,2,32,16,1,128]{5,3,1,4,0,2:T(8,128)}), f32[1,2,32,16,1,128]{5,3,1,4,0,2:T(8,128)S(1)}, u32[]{:S(2)}, u32[]{:S(2)}) async-start(f32[1,2,32,16,1,128]{5,3,1,4,0,2:T(8,128)} %copy.43), calls=%async_computation.1 | async-start | bytes 1048576 | tf_op jit(solution)/shard_map/all_to_all | solution.py:92
  131.9 17.6 %copy-start.1 = (f32[1,2,16,4096]{3,2,1,0:T(8,128)S(1)}, f32[1,2,16,4096]{3,2,1,0:T(8,128)}, u32[]{:S(2)}) copy-start(f32[1,2,16,4096]{3,2,1,0:T(8,128)} %param.8) | copy-start | bytes 1572868
  133.0 10.1 %collective-permute-start.10 = (bf16[2,512,128]{2,1,0:T(8,128)(2,1)}, bf16[2,512,128]{2,1,0:T(8,128)(2,1)}, u32[]{:S(2)}, u32[]{:S(2)}) collective-permute-start(bf16[2,512,128]{2,1,0:T(8,128)(2,1)} %collective-permute-done.8), channel_id=1, source_target_pairs={{0,64},{32,96},{64,128},{96,160},{128,192},{160,224},{192,0},{224,... | collective-permute-start | bytes 786440 | tf_op jit(solution)/shard_map/ppermute | solution.py:49
  133.3 9.8 %collective-permute-start.11 = (bf16[2,512,128]{2,1,0:T(8,128)(2,1)}, bf16[2,512,128]{2,1,0:T(8,128)(2,1)S(1)}, u32[]{:S(2)}, u32[]{:S(2)}) collective-permute-start(bf16[2,512,128]{2,1,0:T(8,128)(2,1)} %collective-permute-done.9), channel_id=1, source_target_pairs={{0,192},{32,224},{64,0},{96,32},{128,64},{160,96},{192,128},{224,1... | collective-permute-start | bytes 786440 | tf_op jit(solution)/shard_map/ppermute | solution.py:50
  143.1 9.9 %collective-permute-start.12 = (bf16[2,512,128]{2,1,0:T(8,128)(2,1)}, bf16[2,512,128]{2,1,0:T(8,128)(2,1)}, u32[]{:S(2)}, u32[]{:S(2)}) collective-permute-start(bf16[2,512,128]{2,1,0:T(8,128)(2,1)} %collective-permute-done.10), channel_id=1, source_target_pairs={{0,64},{32,96},{64,128},{96,160},{128,192},{160,224},{192,0},{224,... | collective-permute-start | bytes 786440 | tf_op jit(solution)/shard_map/ppermute | solution.py:49
  143.2 11.1 %collective-permute-start.13 = (bf16[2,512,128]{2,1,0:T(8,128)(2,1)S(1)}, bf16[2,512,128]{2,1,0:T(8,128)(2,1)}, u32[]{:S(2)}, u32[]{:S(2)}) collective-permute-start(bf16[2,512,128]{2,1,0:T(8,128)(2,1)S(1)} %collective-permute-done.11), channel_id=1, source_target_pairs={{0,192},{32,224},{64,0},{96,32},{128,64},{160,96},{192,128},{224,1... | collective-permute-start | bytes 786440 | tf_op jit(solution)/shard_map/ppermute | solution.py:50
  155.2 1.3 copy-start
Sparse Core Ops, SparseCore 0:
  26.4 82.7 reduce-scatter.1
where the time goes:
time: 165 us; the launch traced here: 163 us
  waiting for transfers between devices  72.9 us (44%)
  starting transfers between devices  42.3 us (26%)
  local copies, waits for them, and re-layouts  19.5 us (12%)
  between operations  15.7 us (10%)
  other arithmetic  12.9 us (8%)
    reduce_scatter x1, waiting for transfers between devices, _step(): lax.psum_scatter(local[:, :, ringed:].reshape(lead, -1, panel_cols), 'dp'...  29.6 us
    ppermute x3, waiting for transfers between devices, _reduce_scatter_dp(): up = lax.ppermute(up, 'dp', plus)  25.3 us
    all_to_all x1, starting transfers between devices, _step(): lax.all_to_all(state, 'shard', split_axis=5, concat_axis=3, tiled=True)  9.7 us
    ppermute x3, starting transfers between devices, _all_gather_dp(): down = lax.ppermute(down, 'dp', minus)  8.59 us
    all_to_all x1, starting transfers between devices, _step(): lax.all_to_all(moved, 'shard', split_axis=2, concat_axis=4, tiled=True)  7.67 us
    ppermute x3, starting transfers between devices, _reduce_scatter_dp(): down = lax.ppermute(down, 'dp', minus)  5.9 us
    ppermute x1, waiting for transfers between devices, _all_gather_dp(): other = lax.ppermute(mine, 'dp', partner)  5.85 us
    ppermute x1, waiting for transfers between devices, _reduce_scatter_dp(): return keep + lax.ppermute(send, 'dp', partner)  5.67 us
  transfers between devices with their start and end apart: 17, of which 8 were waited for; matrix products, arithmetic and copies ran while one was open for 14% of the time, Pallas kernels for 0%

commit v1 on v0

--- a/solution.py
+++ b/solution.py
@@ -80,10 +80,7 @@
     state = lax.all_to_all(state, "shard", split_axis=5, concat_axis=3, tiled=True)
     state = state.reshape(3, relations, 2, block, panel_cols)
     local = grads.reshape(lead, groups, block, panel_cols)
-    ringed = block * 5 // 8
-    offload = lax.psum_scatter(local[:, :, ringed:].reshape(lead, -1, panel_cols), "dp", scatter_dimension=1, tiled=True)
-    summed = _reduce_scatter_dp(local[:, :, :ringed], groups)
-    summed = jnp.concatenate([summed, offload], axis=1)
+    summed = _reduce_scatter_dp(local, groups)
     gradient = summed.reshape(relations, 2, block, panel_cols) / groups
     fresh, _, _ = _adam(gradient, state[0], state[1], state[2], learn, fix_one, fix_two)
     fresh = fresh.astype(jnp.bfloat16).reshape(lead, block, panel_cols)

time: 165 us -> 128 us (0.78)
  waiting for transfers between devices: 72.9 us -> 53 us
  between operations: 15.7 us -> 2.28 us
  local copies, waits for them, and re-layouts: 19.5 us -> 13.9 us
  other arithmetic: 12.9 us -> 14.7 us
    reduce_scatter x1 -> x0, waiting for transfers between devices: 29.6 us -> none  [_step(): lax.psum_scatter(local[:, :, ringed:].reshape(lead, -1, panel_cols), 'dp'...]
    ppermute x3, waiting for transfers between devices: 25.3 us -> 33.3 us  [_reduce_scatter_dp(): up = lax.ppermute(up, 'dp', plus)]
    slice x2 -> x0, local copies, waits for them, and re-layouts: 4.65 us -> none  [the longest x1 2.72 us: _step(): local[:, :, ringed:].reshape(lead, -1, panel_cols)]
    ppermute x1, waiting for transfers between devices: 5.67 us -> 7.91 us  [_reduce_scatter_dp(): return keep + lax.ppermute(send, 'dp', partner)]
    select_n x1, other arithmetic: 0.06 us -> 2.09 us  [_reduce_scatter_dp(): send = lax.select(h == 0, down, up)]
    unnamed x13 -> x11, local copies, waits for them, and re-layouts: 3.76 us -> 3.76 us
  transfers between devices with their start and end apart: 17 -> 16, of which waited for: 8 -> 8; matrix products, arithmetic and copies ran while one was open for 14% -> 15% of each run, Pallas kernels for 0% -> 0%
where the time goes in v1:
time: 128 us; the launch traced here: 127 us
  waiting for transfers between devices  53 us (41%)
  starting transfers between devices  43.3 us (34%)
  other arithmetic  14.7 us (11%)
  local copies, waits for them, and re-layouts  13.9 us (11%)
  between operations  2.28 us (2%)
    ppermute x3, waiting for transfers between devices, _reduce_scatter_dp(): up = lax.ppermute(up, 'dp', plus)  33.3 us
    all_to_all x1, starting transfers between devices, _step(): lax.all_to_all(state, 'shard', split_axis=5, concat_axis=3, tiled=True)  9.65 us
    ppermute x3, starting transfers between devices, _all_gather_dp(): down = lax.ppermute(down, 'dp', minus)  9.38 us
    all_to_all x1, starting transfers between devices, _step(): lax.all_to_all(moved, 'shard', split_axis=2, concat_axis=4, tiled=True)  8.33 us
    ppermute x1, waiting for transfers between devices, _reduce_scatter_dp(): return keep + lax.ppermute(send, 'dp', partner)  7.91 us
    ppermute x3, starting transfers between devices, _reduce_scatter_dp(): down = lax.ppermute(down, 'dp', minus)  5.3 us
    ppermute x1, waiting for transfers between devices, _all_gather_dp(): other = lax.ppermute(mine, 'dp', partner)  5.15 us
    ppermute x3, waiting for transfers between devices, _all_gather_dp(): up = lax.ppermute(up, 'dp', plus)  4.64 us
  transfers between devices with their start and end apart: 16, of which 8 were waited for; matrix products, arithmetic and copies ran while one was open for 15% of the time, Pallas kernels for 0%

profile of v1, /device:TPU:32, one launch (start us, length us, event | category | flops | bytes accessed | tf_op | source)
XLA Modules:
  0.0 127.2 jit_solution(3362578774479288009)
XLA Ops:
  3.3 2.1 %copy.64 = f32[3,1,2,1,16,32,128]{6,4,2,3,1,0,5:T(8,128)} copy(f32[3,1,2,1,16,32,128]{6,5,0,4,2,3,1:T(8,128)S(1)} %pad_maximum_fusion) | data formatting | bytes 3145728 | tf_op jit(solution)/shard_map/stack | solution.py:79
  5.3 9.7 %all-to-all-start.1 = ((f32[3,1,2,1,16,32,128]{6,4,2,3,1,0,5:T(8,128)}), f32[3,1,2,1,16,32,128]{6,4,2,3,1,0,5:T(8,128)S(1)}, u32[]{:S(2)}, u32[]{:S(2)}) async-start(f32[3,1,2,1,16,32,128]{6,4,2,3,1,0,5:T(8,128)} %copy.64), calls=%async_computation.1 | async-start | bytes 3145728 | tf_op jit(solution)/shard_map/all_to_all | solution.py:80
  16.3 1.7 %collective-permute-start = (f32[2,512,128]{2,1,0:T(8,128)S(1)}, f32[2,512,128]{2,1,0:T(8,128)S(1)}, u32[]{:S(2)}, u32[]{:S(2)}) collective-permute-start(f32[2,512,128]{2,1,0:T(8,128)S(1)} %get-tuple-element.18), channel_id=1, source_target_pairs={{0,64},{32,96},{64,128},{96,160},{128,192},{160,224},{192,0},{224,... | collective-permute-start | bytes 1572872 | tf_op jit(solution)/shard_map/ppermute | solution.py:27
  18.0 1.7 %collective-permute-start.3 = (f32[2,512,128]{2,1,0:T(8,128)S(1)}, f32[2,512,128]{2,1,0:T(8,128)}, u32[]{:S(2)}, u32[]{:S(2)}) collective-permute-start(f32[2,512,128]{2,1,0:T(8,128)S(1)} %get-tuple-element.17), channel_id=1, source_target_pairs={{0,192},{32,224},{64,0},{96,32},{128,64},{160,96},{192,128},{224,1... | collective-permute-start | bytes 1572872 | tf_op jit(solution)/shard_map/ppermute | solution.py:28
  19.6 12.0 %collective-permute-done = f32[2,512,128]{2,1,0:T(8,128)S(1)} collective-permute-done((f32[2,512,128]{2,1,0:T(8,128)S(1)}, f32[2,512,128]{2,1,0:T(8,128)S(1)}, u32[]{:S(2)}, u32[]{:S(2)}) %collective-permute-start) | collective-permute-done | bytes 524320 | tf_op jit(solution)/shard_map/ppermute | solution.py:27
  33.2 1.7 %collective-permute-start.1 = (f32[2,512,128]{2,1,0:T(8,128)S(1)}, f32[2,512,128]{2,1,0:T(8,128)S(1)}, u32[]{:S(2)}, u32[]{:S(2)}) collective-permute-start(f32[2,512,128]{2,1,0:T(8,128)S(1)} %get-tuple-element.16), channel_id=1, source_target_pairs={{0,64},{32,96},{64,128},{96,160},{128,192},{160,224},{192,0},{224,... | collective-permute-start | bytes 1572872 | tf_op jit(solution)/shard_map/ppermute | solution.py:27
  34.9 1.7 %collective-permute-start.4 = (f32[2,512,128]{2,1,0:T(8,128)S(1)}, f32[2,512,128]{2,1,0:T(8,128)}, u32[]{:S(2)}, u32[]{:S(2)}) collective-permute-start(f32[2,512,128]{2,1,0:T(8,128)S(1)} %get-tuple-element.15), channel_id=1, source_target_pairs={{0,192},{32,224},{64,0},{96,32},{128,64},{160,96},{192,128},{224,1... | collective-permute-start | bytes 1572872 | tf_op jit(solution)/shard_map/ppermute | solution.py:28
  36.5 11.0 %collective-permute-done.1 = f32[2,512,128]{2,1,0:T(8,128)S(1)} collective-permute-done((f32[2,512,128]{2,1,0:T(8,128)S(1)}, f32[2,512,128]{2,1,0:T(8,128)S(1)}, u32[]{:S(2)}, u32[]{:S(2)}) %collective-permute-start.1) | collective-permute-done | bytes 524320 | tf_op jit(solution)/shard_map/ppermute | solution.py:27
  47.5 2.3 %bitcast_add_fusion.1 = (f32[2,512,128]{2,1,0:T(8,128)S(1)}, f32[2,512,128]{2,1,0:T(8,128)}) fusion(f32[2,512,128]{2,1,0:T(8,128)} %collective-permute-done.4, f32[2,8,512,128]{3,2,1,0:T(8,128)} %bitcast.102, s32[]{:T(128)S(6)} %select_n.138, f32[2,512,128]{2,1,0:T(8,128)S(1)} %collective-permute-done.1, s32[]{:T(128)S(6)} %select_n.130), kind=kLoop, calls=%fused_computation.9 | loop fusion | flops 262144 | bytes 3145736 | tf_op jit(solution)/shard_map/add | solution.py:30
  51.1 2.0 %collective-permute-start.5 = (f32[2,512,128]{2,1,0:T(8,128)S(1)}, f32[2,512,128]{2,1,0:T(8,128)S(1)}, u32[]{:S(2)}, u32[]{:S(2)}) collective-permute-start(f32[2,512,128]{2,1,0:T(8,128)S(1)} %get-tuple-element.13), channel_id=1, source_target_pairs={{0,192},{32,224},{64,0},{96,32},{128,64},{160,96},{192,128},{224,1... | collective-permute-start | bytes 1572872 | tf_op jit(solution)/shard_map/ppermute | solution.py:28
  53.0 10.4 %collective-permute-done.2 = f32[2,512,128]{2,1,0:T(8,128)S(1)} collective-permute-done((f32[2,512,128]{2,1,0:T(8,128)}, f32[2,512,128]{2,1,0:T(8,128)S(1)}, u32[]{:S(2)}, u32[]{:S(2)}) %collective-permute-start.2) | collective-permute-done | bytes 524320 | tf_op jit(solution)/shard_map/ppermute | solution.py:27
  63.4 2.1 %broadcast_select_fusion.2 = f32[2,512,128]{2,1,0:T(8,128)} fusion(pred[]{:T(512)S(6)} %eq.37, f32[2,512,128]{2,1,0:T(8,128)S(1)} %collective-permute-done.2, f32[2,8,512,128]{3,2,1,0:T(8,128)} %bitcast.103, s32[]{:T(128)S(6)} %select_n.132, f32[2,512,128]{2,1,0:T(8,128)S(1)} %collective-permute-done.5, s32[]{:T(128)S(6)} %select_n.140), kind=kLoop, calls=%fused_computation.29 | loop fusion | flops 393216 | bytes 2621449 | tf_op jit(solution)/shard_map/select_n | solution.py:32
  65.5 2.7 %collective-permute-start.6 = (f32[2,512,128]{2,1,0:T(8,128)}, f32[2,512,128]{2,1,0:T(8,128)S(1)}, u32[]{:S(2)}, u32[]{:S(2)}) collective-permute-start(f32[2,512,128]{2,1,0:T(8,128)} %broadcast_select_fusion.2), channel_id=1, source_target_pairs={{0,32},{32,0},{64,96},{96,64},{128,160},{160,128},{192,224},{224,1... | collective-permute-start | bytes 1572872 | tf_op jit(solution)/shard_map/ppermute | solution.py:33
  70.6 7.9 %collective-permute-done.6 = f32[2,512,128]{2,1,0:T(8,128)S(1)} collective-permute-done((f32[2,512,128]{2,1,0:T(8,128)}, f32[2,512,128]{2,1,0:T(8,128)S(1)}, u32[]{:S(2)}, u32[]{:S(2)}) %collective-permute-start.6) | collective-permute-done | bytes 524320 | tf_op jit(solution)/shard_map/ppermute | solution.py:33
  78.5 2.4 %subtract_convert_fusion = (bf16[2,512,128]{2,1,0:T(8,128)(2,1)S(1)}, f32[2,512,128]{2,1,0:T(8,128)S(1)}) fusion(f32[2,512,128]{2,1,0:T(8,128)S(1)} %bitcast.109, f32[2,512,128]{2,1,0:T(8,128)S(1)} %bitcast.108, f32[2,512,128]{2,1,0:T(8,128)S(1)} %bitcast.107, f32[]{:T(128)} %bitcast.15, f32[]{:T(128)} %bitcast.14, f32[]{:T(128)} %fusion.2, ...), kind=kLoop, calls=%fused_computation.14 | loop fusion | flops 2490368 | bytes 4980757 | tf_op jit(solution)/shard_map/convert_element_type | solution.py:86
  80.9 2.8 %collective-permute-start.7 = (bf16[2,512,128]{2,1,0:T(8,128)(2,1)S(1)}, bf16[2,512,128]{2,1,0:T(8,128)(2,1)S(1)}, u32[]{:S(2)}, u32[]{:S(2)}) collective-permute-start(bf16[2,512,128]{2,1,0:T(8,128)(2,1)S(1)} %get-tuple-element.8), channel_id=1, source_target_pairs={{0,32},{32,0},{64,96},{96,64},{128,160},{160,128},{192,224},{224,1... | collective-permute-start | bytes 786440 | tf_op jit(solution)/shard_map/ppermute | solution.py:41
  83.7 5.1 %collective-permute-done.7 = bf16[2,512,128]{2,1,0:T(8,128)(2,1)S(1)} collective-permute-done((bf16[2,512,128]{2,1,0:T(8,128)(2,1)S(1)}, bf16[2,512,128]{2,1,0:T(8,128)(2,1)S(1)}, u32[]{:S(2)}, u32[]{:S(2)}) %collective-permute-start.7) | collective-permute-done | bytes 262176 | tf_op jit(solution)/shard_map/ppermute | solution.py:41
  89.9 2.9 %collective-permute-start.9 = (bf16[2,512,128]{2,1,0:T(8,128)(2,1)S(1)}, bf16[2,512,128]{2,1,0:T(8,128)(2,1)}, u32[]{:S(2)}, u32[]{:S(2)}) collective-permute-start(bf16[2,512,128]{2,1,0:T(8,128)(2,1)S(1)} %get-tuple-element.23), channel_id=1, source_target_pairs={{0,192},{32,224},{64,0},{96,32},{128,64},{160,96},{192,128},{224,1... | collective-permute-start | bytes 786440 | tf_op jit(solution)/shard_map/ppermute | solution.py:50
  93.7 8.3 %all-to-all-start = ((f32[1,2,32,16,1,128]{5,3,1,4,0,2:T(8,128)}), f32[1,2,32,16,1,128]{5,3,1,4,0,2:T(8,128)S(1)}, u32[]{:S(2)}, u32[]{:S(2)}) async-start(f32[1,2,32,16,1,128]{5,3,1,4,0,2:T(8,128)} %copy.59), calls=%async_computation | async-start | bytes 1048576 | tf_op jit(solution)/shard_map/all_to_all | solution.py:89
  103.9 3.2 %collective-permute-start.11 = (bf16[2,512,128]{2,1,0:T(8,128)(2,1)}, bf16[2,512,128]{2,1,0:T(8,128)(2,1)S(1)}, u32[]{:S(2)}, u32[]{:S(2)}) collective-permute-start(bf16[2,512,128]{2,1,0:T(8,128)(2,1)} %collective-permute-done.9), channel_id=1, source_target_pairs={{0,192},{32,224},{64,0},{96,32},{128,64},{160,96},{192,128},{224,1... | collective-permute-start | bytes 786440 | tf_op jit(solution)/shard_map/ppermute | solution.py:50
  109.1 4.6 %collective-permute-done.10 = bf16[2,512,128]{2,1,0:T(8,128)(2,1)} collective-permute-done((bf16[2,512,128]{2,1,0:T(8,128)(2,1)}, bf16[2,512,128]{2,1,0:T(8,128)(2,1)}, u32[]{:S(2)}, u32[]{:S(2)}) %collective-permute-start.10) | collective-permute-done | bytes 262176 | tf_op jit(solution)/shard_map/ppermute | solution.py:49
  113.7 3.2 %collective-permute-start.13 = (bf16[2,512,128]{2,1,0:T(8,128)(2,1)S(1)}, bf16[2,512,128]{2,1,0:T(8,128)(2,1)}, u32[]{:S(2)}, u32[]{:S(2)}) collective-permute-start(bf16[2,512,128]{2,1,0:T(8,128)(2,1)S(1)} %collective-permute-done.11), channel_id=1, source_target_pairs={{0,192},{32,224},{64,0},{96,32},{128,64},{160,96},{192,128},{224,1... | collective-permute-start | bytes 786440 | tf_op jit(solution)/shard_map/ppermute | solution.py:50
  118.0 1.8 %all-to-all-done = f32[1,2,32,16,1,128]{5,3,1,4,0,2:T(8,128)S(1)} async-done(((f32[1,2,32,16,1,128]{5,3,1,4,0,2:T(8,128)}), f32[1,2,32,16,1,128]{5,3,1,4,0,2:T(8,128)S(1)}, u32[]{:S(2)}, u32[]{:S(2)}) %all-to-all-start) | async-done | bytes 524320 | tf_op jit(solution)/shard_map/all_to_all | solution.py:89
  120.1 3.6 %multiply_subtract_fusion = (f32[1,2,16,4096]{3,2,1,0:T(8,128)}, f32[1,2,16,4096]{3,2,1,0:T(8,128)}, f32[1,2,16,4096]{3,2,1,0:T(8,128)}) fusion(f32[1,2,16,4096]{3,2,1,0:T(8,128)S(1)} %copy-done.1, f32[]{:T(128)} %bitcast.15, f32[]{:T(128)} %bitcast.14, f32[]{:T(128)} %fusion.2, f32[1,2,16,4096]{3,0,2,1:T(1,128)S(1)} %bitcast.114, ...), kind=kLoop, calls=%fused_computation.15 | loop fusion | flops 1966080 | bytes 3670028 | tf_op jit(solution)/shard_map/sub | solution.py:60
  (43 shorter events, 18.2 us)
Async XLA Ops:
  0.6 2.4 %copy-start.2 = (f32[1,2,16,4096]{3,2,1,0:T(8,128)S(1)}, f32[1,2,16,4096]{3,2,1,0:T(8,128)}, u32[]{:S(2)}) copy-start(f32[1,2,16,4096]{3,2,1,0:T(8,128)} %param.10) | copy-start | bytes 1572868
  5.3 65.0 %all-to-all-start.1 = ((f32[3,1,2,1,16,32,128]{6,4,2,3,1,0,5:T(8,128)}), f32[3,1,2,1,16,32,128]{6,4,2,3,1,0,5:T(8,128)S(1)}, u32[]{:S(2)}, u32[]{:S(2)}) async-start(f32[3,1,2,1,16,32,128]{6,4,2,3,1,0,5:T(8,128)} %copy.64), calls=%async_computation.1 | async-start | bytes 3145728 | tf_op jit(solution)/shard_map/all_to_all | solution.py:80
  16.3 15.3 %collective-permute-start = (f32[2,512,128]{2,1,0:T(8,128)S(1)}, f32[2,512,128]{2,1,0:T(8,128)S(1)}, u32[]{:S(2)}, u32[]{:S(2)}) collective-permute-start(f32[2,512,128]{2,1,0:T(8,128)S(1)} %get-tuple-element.18), channel_id=1, source_target_pairs={{0,64},{32,96},{64,128},{96,160},{128,192},{160,224},{192,0},{224,... | collective-permute-start | bytes 1572872 | tf_op jit(solution)/shard_map/ppermute | solution.py:27
  18.0 13.8 %collective-permute-start.3 = (f32[2,512,128]{2,1,0:T(8,128)S(1)}, f32[2,512,128]{2,1,0:T(8,128)}, u32[]{:S(2)}, u32[]{:S(2)}) collective-permute-start(f32[2,512,128]{2,1,0:T(8,128)S(1)} %get-tuple-element.17), channel_id=1, source_target_pairs={{0,192},{32,224},{64,0},{96,32},{128,64},{160,96},{192,128},{224,1... | collective-permute-start | bytes 1572872 | tf_op jit(solution)/shard_map/ppermute | solution.py:28
  33.2 14.3 %collective-permute-start.1 = (f32[2,512,128]{2,1,0:T(8,128)S(1)}, f32[2,512,128]{2,1,0:T(8,128)S(1)}, u32[]{:S(2)}, u32[]{:S(2)}) collective-permute-start(f32[2,512,128]{2,1,0:T(8,128)S(1)} %get-tuple-element.16), channel_id=1, source_target_pairs={{0,64},{32,96},{64,128},{96,160},{128,192},{160,224},{192,0},{224,... | collective-permute-start | bytes 1572872 | tf_op jit(solution)/shard_map/ppermute | solution.py:27
  34.9 12.7 %collective-permute-start.4 = (f32[2,512,128]{2,1,0:T(8,128)S(1)}, f32[2,512,128]{2,1,0:T(8,128)}, u32[]{:S(2)}, u32[]{:S(2)}) collective-permute-start(f32[2,512,128]{2,1,0:T(8,128)S(1)} %get-tuple-element.15), channel_id=1, source_target_pairs={{0,192},{32,224},{64,0},{96,32},{128,64},{160,96},{192,128},{224,1... | collective-permute-start | bytes 1572872 | tf_op jit(solution)/shard_map/ppermute | solution.py:28
  49.8 19.8 %copy-start.3 = (f32[64]{0:T(128)S(1)}, f32[64]{0:T(128)}, u32[]{:S(2)}) copy-start(f32[64]{0:T(128)} %param.12) | copy-start | bytes 772
  49.8 13.6 %collective-permute-start.2 = (f32[2,512,128]{2,1,0:T(8,128)}, f32[2,512,128]{2,1,0:T(8,128)S(1)}, u32[]{:S(2)}, u32[]{:S(2)}) collective-permute-start(f32[2,512,128]{2,1,0:T(8,128)} %get-tuple-element.14), channel_id=1, source_target_pairs={{0,64},{32,96},{64,128},{96,160},{128,192},{160,224},{192,0},{224,... | collective-permute-start | bytes 1572872 | tf_op jit(solution)/shard_map/ppermute | solution.py:27
  51.1 12.3 %collective-permute-start.5 = (f32[2,512,128]{2,1,0:T(8,128)S(1)}, f32[2,512,128]{2,1,0:T(8,128)S(1)}, u32[]{:S(2)}, u32[]{:S(2)}) collective-permute-start(f32[2,512,128]{2,1,0:T(8,128)S(1)} %get-tuple-element.13), channel_id=1, source_target_pairs={{0,192},{32,224},{64,0},{96,32},{128,64},{160,96},{192,128},{224,1... | collective-permute-start | bytes 1572872 | tf_op jit(solution)/shard_map/ppermute | solution.py:28
  65.5 13.0 %collective-permute-start.6 = (f32[2,512,128]{2,1,0:T(8,128)}, f32[2,512,128]{2,1,0:T(8,128)S(1)}, u32[]{:S(2)}, u32[]{:S(2)}) collective-permute-start(f32[2,512,128]{2,1,0:T(8,128)} %broadcast_select_fusion.2), channel_id=1, source_target_pairs={{0,32},{32,0},{64,96},{96,64},{128,160},{160,128},{192,224},{224,1... | collective-permute-start | bytes 1572872 | tf_op jit(solution)/shard_map/ppermute | solution.py:33
  80.9 8.0 %collective-permute-start.7 = (bf16[2,512,128]{2,1,0:T(8,128)(2,1)S(1)}, bf16[2,512,128]{2,1,0:T(8,128)(2,1)S(1)}, u32[]{:S(2)}, u32[]{:S(2)}) collective-permute-start(bf16[2,512,128]{2,1,0:T(8,128)(2,1)S(1)} %get-tuple-element.8), channel_id=1, source_target_pairs={{0,32},{32,0},{64,96},{96,64},{128,160},{160,128},{192,224},{224,1... | collective-permute-start | bytes 786440 | tf_op jit(solution)/shard_map/ppermute | solution.py:41
  89.6 14.0 %collective-permute-start.8 = (bf16[2,512,128]{2,1,0:T(8,128)(2,1)}, bf16[2,512,128]{2,1,0:T(8,128)(2,1)}, u32[]{:S(2)}, u32[]{:S(2)}) collective-permute-start(bf16[2,512,128]{2,1,0:T(8,128)(2,1)} %get-tuple-element.22), channel_id=1, source_target_pairs={{0,64},{32,96},{64,128},{96,160},{128,192},{160,224},{192,0},{224,... | collective-permute-start | bytes 786440 | tf_op jit(solution)/shard_map/ppermute | solution.py:49
  89.9 14.0 %collective-permute-start.9 = (bf16[2,512,128]{2,1,0:T(8,128)(2,1)S(1)}, bf16[2,512,128]{2,1,0:T(8,128)(2,1)}, u32[]{:S(2)}, u32[]{:S(2)}) collective-permute-start(bf16[2,512,128]{2,1,0:T(8,128)(2,1)S(1)} %get-tuple-element.23), channel_id=1, source_target_pairs={{0,192},{32,224},{64,0},{96,32},{128,64},{160,96},{192,128},{224,1... | collective-permute-start | bytes 786440 | tf_op jit(solution)/shard_map/ppermute | solution.py:50
  93.7 26.1 %all-to-all-start = ((f32[1,2,32,16,1,128]{5,3,1,4,0,2:T(8,128)}), f32[1,2,32,16,1,128]{5,3,1,4,0,2:T(8,128)S(1)}, u32[]{:S(2)}, u32[]{:S(2)}) async-start(f32[1,2,32,16,1,128]{5,3,1,4,0,2:T(8,128)} %copy.59), calls=%async_computation | async-start | bytes 1048576 | tf_op jit(solution)/shard_map/all_to_all | solution.py:89
  102.5 17.6 %copy-start.1 = (f32[1,2,16,4096]{3,2,1,0:T(8,128)S(1)}, f32[1,2,16,4096]{3,2,1,0:T(8,128)}, u32[]{:S(2)}) copy-start(f32[1,2,16,4096]{3,2,1,0:T(8,128)} %param.8) | copy-start | bytes 1572868
  103.6 10.1 %collective-permute-start.10 = (bf16[2,512,128]{2,1,0:T(8,128)(2,1)}, bf16[2,512,128]{2,1,0:T(8,128)(2,1)}, u32[]{:S(2)}, u32[]{:S(2)}) collective-permute-start(bf16[2,512,128]{2,1,0:T(8,128)(2,1)} %collective-permute-done.8), channel_id=1, source_target_pairs={{0,64},{32,96},{64,128},{96,160},{128,192},{160,224},{192,0},{224,... | collective-permute-start | bytes 786440 | tf_op jit(solution)/shard_map/ppermute | solution.py:49
  103.9 9.8 %collective-permute-start.11 = (bf16[2,512,128]{2,1,0:T(8,128)(2,1)}, bf16[2,512,128]{2,1,0:T(8,128)(2,1)S(1)}, u32[]{:S(2)}, u32[]{:S(2)}) collective-permute-start(bf16[2,512,128]{2,1,0:T(8,128)(2,1)} %collective-permute-done.9), channel_id=1, source_target_pairs={{0,192},{32,224},{64,0},{96,32},{128,64},{160,96},{192,128},{224,1... | collective-permute-start | bytes 786440 | tf_op jit(solution)/shard_map/ppermute | solution.py:50
  113.7 10.0 %collective-permute-start.12 = (bf16[2,512,128]{2,1,0:T(8,128)(2,1)}, bf16[2,512,128]{2,1,0:T(8,128)(2,1)}, u32[]{:S(2)}, u32[]{:S(2)}) collective-permute-start(bf16[2,512,128]{2,1,0:T(8,128)(2,1)} %collective-permute-done.10), channel_id=1, source_target_pairs={{0,64},{32,96},{64,128},{96,160},{128,192},{160,224},{192,0},{224,... | collective-permute-start | bytes 786440 | tf_op jit(solution)/shard_map/ppermute | solution.py:49
  113.7 11.2 %collective-permute-start.13 = (bf16[2,512,128]{2,1,0:T(8,128)(2,1)S(1)}, bf16[2,512,128]{2,1,0:T(8,128)(2,1)}, u32[]{:S(2)}, u32[]{:S(2)}) collective-permute-start(bf16[2,512,128]{2,1,0:T(8,128)(2,1)S(1)} %collective-permute-done.11), channel_id=1, source_target_pairs={{0,192},{32,224},{64,0},{96,32},{128,64},{160,96},{192,128},{224,1... | collective-permute-start | bytes 786440 | tf_op jit(solution)/shard_map/ppermute | solution.py:50
  125.9 1.3 %copy-start = (bf16[2,4,2,512,128]{4,3,2,1,0:T(8,128)(2,1)}, bf16[2,4,2,512,128]{4,3,2,1,0:T(8,128)(2,1)S(1)}, u32[]{:S(2)}) copy-start(bf16[2,4,2,512,128]{4,3,2,1,0:T(8,128)(2,1)S(1)} %bitcast_dynamic-update-slice_fusion) | copy-start | bytes 6291460

commit v2 on v1

--- a/solution.py
+++ b/solution.py
@@ -16,21 +16,35 @@
     return lax.dynamic_index_in_dim(x, index, axis=1, keepdims=False)
 
 
+def _ring_sum(y, ring, perm, sign, pick):
+    acc = pick((y - sign) % ring)
+    for t in range(ring - 1):
+        acc = lax.ppermute(acc, "dp", perm)
+        acc = acc + pick((y - sign * (t + 2)) % ring)
+    return acc
+
+
 def _reduce_scatter_dp(x, groups):
     ring, plus, minus, partner = _dp_rings(groups)
     d = lax.axis_index("dp")
     y = d // 2
     h = d % 2
-    up = _take(x, 2 * ((y - 1) % ring))
-    down = _take(x, 2 * ((y + 1) % ring) + 1)
-    for t in range(ring - 1):
-        up = lax.ppermute(up, "dp", plus)
-        down = lax.ppermute(down, "dp", minus)
-        up = up + _take(x, 2 * ((y - t - 2) % ring))
-        down = down + _take(x, 2 * ((y + t + 2) % ring) + 1)
+    half = x.shape[0] // 2
+    rows = x.shape[2] // 2
+    first = x[:half]
+    up = _ring_sum(y, ring, plus, 1, lambda c: _take(first, 2 * c))
+    down = _ring_sum(y, ring, minus, -1, lambda c: _take(first, 2 * c + 1))
     keep = lax.select(h == 0, up, down)
     send = lax.select(h == 0, down, up)
-    return keep + lax.ppermute(send, "dp", partner)
+    done_first = keep + lax.ppermute(send, "dp", partner)
+    second = x[half:].reshape(x.shape[0] - half, ring, 2, x.shape[2], x.shape[3])
+    mine = lax.dynamic_index_in_dim(second, h, axis=2, keepdims=False)
+    theirs = lax.dynamic_index_in_dim(second, 1 - h, axis=2, keepdims=False)
+    paired = mine + lax.ppermute(theirs, "dp", partner)
+    top = _ring_sum(y, ring, plus, 1, lambda c: _take(paired, c)[:, :rows])
+    bottom = _ring_sum(y, ring, minus, -1, lambda c: _take(paired, c)[:, rows:])
+    done_second = jnp.concatenate([top, bottom], axis=1)
+    return jnp.concatenate([done_first, done_second], axis=0)
 
 
 def _all_gather_dp(mine, groups):

time: 128 us -> 131 us (1.023); the launches traced: 127 us -> 128 us
  starting transfers between devices: 43.3 us -> 57.3 us
  waiting for transfers between devices: 53 us -> 41.6 us
  other arithmetic: 14.7 us -> 13 us
    ppermute x7 -> x14, waiting for transfers between devices: 41.4 us -> 19.3 us  [the longest x12 13.3 us: _ring_sum(): acc = lax.ppermute(acc, 'dp', perm)]
    ppermute x7 -> x14, starting transfers between devices: 12.6 us -> 25.8 us  [the longest x12 20 us: _ring_sum(): acc = lax.ppermute(acc, 'dp', perm)]
    all_to_all x1, waiting for transfers between devices: 1.83 us -> 9.45 us  [_step(): lax.all_to_all(moved, 'shard', split_axis=2, concat_axis=4, tiled=True)]
    ppermute x1, waiting for transfers between devices: 5.15 us -> 0.1 us  [_all_gather_dp(): other = lax.ppermute(mine, 'dp', partner)]
    ppermute x3, waiting for transfers between devices: 4.64 us -> 8.7 us  [_all_gather_dp(): up = lax.ppermute(up, 'dp', plus)]
    ppermute x3, waiting for transfers between devices: 0.01 us -> 4.01 us  [_all_gather_dp(): down = lax.ppermute(down, 'dp', minus)]
    slice x0 -> x3, local copies, waits for them, and re-layouts: none -> 3.83 us  [the longest x1 3.81 us: _reduce_scatter_dp(): first = x[:half]]
    dynamic_update_slice x4, local copies, waits for them, and re-layouts: 3.09 us -> 0.25 us  [_all_gather_dp(): lax.dynamic_update_slice(out, up[:, None, None], (0, (y - t - 1) % ring,...]
  transfers between devices with their start and end apart: 16 -> 23, of which waited for: 8 -> 13; matrix products, arithmetic and copies ran while one was open for 15% -> 16% of each run, Pallas kernels for 0% -> 0%
where the time goes in v2:
time: 131 us; the launch traced here: 128 us
  starting transfers between devices  57.3 us (44%)
  waiting for transfers between devices  41.6 us (32%)
  local copies, waits for them, and re-layouts  14.1 us (11%)
  other arithmetic  13 us (10%)
  between operations  2.48 us (2%)
    ppermute x12, starting transfers between devices, _ring_sum(): acc = lax.ppermute(acc, 'dp', perm)  20 us
    ppermute x12, waiting for transfers between devices, _ring_sum(): acc = lax.ppermute(acc, 'dp', perm)  13.3 us
    ppermute x3, starting transfers between devices, _all_gather_dp(): down = lax.ppermute(down, 'dp', minus)  10.7 us
    all_to_all x1, starting transfers between devices, _step(): lax.all_to_all(state, 'shard', split_axis=5, concat_axis=3, tiled=True)  9.7 us
    all_to_all x1, waiting for transfers between devices, _step(): lax.all_to_all(moved, 'shard', split_axis=2, concat_axis=4, tiled=True)  9.45 us
    ppermute x3, waiting for transfers between devices, _all_gather_dp(): up = lax.ppermute(up, 'dp', plus)  8.7 us
    all_to_all x1, starting transfers between devices, _step(): lax.all_to_all(moved, 'shard', split_axis=2, concat_axis=4, tiled=True)  8.21 us
    ppermute x1, waiting for transfers between devices, _reduce_scatter_dp(): done_first = keep + lax.ppermute(send, 'dp', partner)  6.04 us
  transfers between devices with their start and end apart: 23, of which 13 were waited for; matrix products, arithmetic and copies ran while one was open for 16% of the time, Pallas kernels for 0%

profile of v2, /device:TPU:32, one launch (start us, length us, event | category | flops | bytes accessed | tf_op | source)
XLA Modules:
  0.0 128.4 jit_solution(15027793245156216010)
XLA Ops:
  0.7 3.8 %fusion.4 = (f32[1,1,1,4096,128]{4,3,2,1,0:T(8,128)S(1)}, f32[1,1,1,4096,128]{4,3,2,1,0:T(8,128)}) fusion(f32[1,1,2,4096,128]{4,3,2,1,0:T(8,128)} %param.7), kind=kLoop, calls=%fused_computation.50 | loop fusion | bytes 8388608 | tf_op jit(solution)/shard_map/slice | solution.py:34
  8.5 2.3 %dynamic-slice_bitcast_fusion = f32[1,4,512,128]{3,2,1,0:T(8,128)} fusion(f32[1,4,2,512,128]{4,3,2,1,0:T(8,128)} %bitcast.113, s32[]{:T(128)S(6)} %select_n.182), kind=kLoop, calls=%fused_computation.3 | loop fusion | bytes 2097156 | tf_op jit(solution)/shard_map/jit(dynamic_index_in_dim)/squeeze | solution.py:42
  10.8 3.0 %collective-permute-start.7 = (f32[1,4,512,128]{3,2,1,0:T(8,128)}, f32[1,4,512,128]{3,2,1,0:T(8,128)}, u32[]{:S(2)}, u32[]{:S(2)}) collective-permute-start(f32[1,4,512,128]{3,2,1,0:T(8,128)} %dynamic-slice_bitcast_fusion), channel_id=1, source_target_pairs={{0,32},{32,0},{64,96},{96,64},{128,160},{160,128},{192,224},{224,1... | collective-permute-start | bytes 3145736 | tf_op jit(solution)/shard_map/ppermute | solution.py:43
  20.4 2.1 %copy.52 = f32[3,1,2,1,16,32,128]{6,4,2,3,1,0,5:T(8,128)} copy(f32[3,1,2,1,16,32,128]{6,5,0,4,2,3,1:T(8,128)S(1)} %pad_maximum_fusion) | data formatting | bytes 3145728 | tf_op jit(solution)/shard_map/stack | solution.py:93
  22.5 9.7 %all-to-all-start.1 = ((f32[3,1,2,1,16,32,128]{6,4,2,3,1,0,5:T(8,128)}), f32[3,1,2,1,16,32,128]{6,4,2,3,1,0,5:T(8,128)}, u32[]{:S(2)}, u32[]{:S(2)}) async-start(f32[3,1,2,1,16,32,128]{6,4,2,3,1,0,5:T(8,128)} %copy.52), calls=%async_computation.1 | async-start | bytes 3145728 | tf_op jit(solution)/shard_map/all_to_all | solution.py:94
  34.3 3.1 %collective-permute-start.5 = (f32[1,512,128]{2,1,0:T(8,128)}, f32[1,512,128]{2,1,0:T(8,128)}, u32[]{:S(2)}, u32[]{:S(2)}) collective-permute-start(f32[1,512,128]{2,1,0:T(8,128)} %get-tuple-element.13), channel_id=1, source_target_pairs={{0,192},{32,224},{64,0},{96,32},{128,64},{160,96},{192,128},{224,1... | collective-permute-start | bytes 786440 | tf_op jit(solution)/shard_map/ppermute | solution.py:22
  37.4 6.5 %collective-permute-done.2 = f32[1,512,128]{2,1,0:T(8,128)S(1)} collective-permute-done((f32[1,512,128]{2,1,0:T(8,128)}, f32[1,512,128]{2,1,0:T(8,128)S(1)}, u32[]{:S(2)}, u32[]{:S(2)}) %collective-permute-start.2) | collective-permute-done | bytes 262176 | tf_op jit(solution)/shard_map/ppermute | solution.py:22
  45.0 2.8 %collective-permute-start.6 = (f32[1,512,128]{2,1,0:T(8,128)S(1)}, f32[1,512,128]{2,1,0:T(8,128)S(1)}, u32[]{:S(2)}, u32[]{:S(2)}) collective-permute-start(f32[1,512,128]{2,1,0:T(8,128)S(1)} %broadcast_select_fusion.2), channel_id=1, source_target_pairs={{0,32},{32,0},{64,96},{96,64},{128,160},{160,128},{192,224},{224,1... | collective-permute-start | bytes 786440 | tf_op jit(solution)/shard_map/ppermute | solution.py:39
  49.8 3.3 %collective-permute-start.11 = (f32[1,256,128]{2,1,0:T(8,128)S(1)}, f32[1,256,128]{2,1,0:T(8,128)S(1)}, u32[]{:S(2)}, u32[]{:S(2)}) collective-permute-start(f32[1,256,128]{2,1,0:T(8,128)S(1)} %slice.64), channel_id=1, source_target_pairs={{0,192},{32,224},{64,0},{96,32},{128,64},{160,96},{192,128},{224,1... | collective-permute-start | bytes 393224 | tf_op jit(solution)/shard_map/ppermute | solution.py:22
  53.1 6.0 %collective-permute-done.6 = f32[1,512,128]{2,1,0:T(8,128)S(1)} collective-permute-done((f32[1,512,128]{2,1,0:T(8,128)S(1)}, f32[1,512,128]{2,1,0:T(8,128)S(1)}, u32[]{:S(2)}, u32[]{:S(2)}) %collective-permute-start.6) | collective-permute-done | bytes 262176 | tf_op jit(solution)/shard_map/ppermute | solution.py:39
  60.4 3.3 %collective-permute-start.12 = (f32[1,256,128]{2,1,0:T(8,128)S(1)}, f32[1,256,128]{2,1,0:T(8,128)S(1)}, u32[]{:S(2)}, u32[]{:S(2)}) collective-permute-start(f32[1,256,128]{2,1,0:T(8,128)S(1)} %slice_add_fusion.2), channel_id=1, source_target_pairs={{0,192},{32,224},{64,0},{96,32},{128,64},{160,96},{192,128},{224,1... | collective-permute-start | bytes 393224 | tf_op jit(solution)/shard_map/ppermute | solution.py:22
  63.6 2.8 %collective-permute-done.9 = f32[1,256,128]{2,1,0:T(8,128)S(1)} collective-permute-done((f32[1,256,128]{2,1,0:T(8,128)S(1)}, f32[1,256,128]{2,1,0:T(8,128)S(1)}, u32[]{:S(2)}, u32[]{:S(2)}) %collective-permute-start.9) | collective-permute-done | bytes 131104 | tf_op jit(solution)/shard_map/ppermute | solution.py:22
  66.8 3.3 %collective-permute-start.13 = (f32[1,256,128]{2,1,0:T(8,128)S(1)}, f32[1,256,128]{2,1,0:T(8,128)S(1)}, u32[]{:S(2)}, u32[]{:S(2)}) collective-permute-start(f32[1,256,128]{2,1,0:T(8,128)S(1)} %slice_add_fusion.1), channel_id=1, source_target_pairs={{0,192},{32,224},{64,0},{96,32},{128,64},{160,96},{192,128},{224,1... | collective-permute-start | bytes 393224 | tf_op jit(solution)/shard_map/ppermute | solution.py:22
  70.1 2.8 %collective-permute-done.10 = f32[1,256,128]{2,1,0:T(8,128)S(1)} collective-permute-done((f32[1,256,128]{2,1,0:T(8,128)S(1)}, f32[1,256,128]{2,1,0:T(8,128)S(1)}, u32[]{:S(2)}, u32[]{:S(2)}) %collective-permute-start.10) | collective-permute-done | bytes 131104 | tf_op jit(solution)/shard_map/ppermute | solution.py:22
  73.9 8.2 %all-to-all-start = ((f32[1,2,32,16,1,128]{5,3,1,4,0,2:T(8,128)}), f32[1,2,32,16,1,128]{5,3,1,4,0,2:T(8,128)S(1)}, u32[]{:S(2)}, u32[]{:S(2)}) async-start(f32[1,2,32,16,1,128]{5,3,1,4,0,2:T(8,128)} %maximum_multiply_fusion), calls=%async_computation | async-start | bytes 1048576 | tf_op jit(solution)/shard_map/all_to_all | solution.py:103
  87.7 2.7 %collective-permute-start.14 = (bf16[2,512,128]{2,1,0:T(8,128)(2,1)S(1)}, bf16[2,512,128]{2,1,0:T(8,128)(2,1)S(1)}, u32[]{:S(2)}, u32[]{:S(2)}) collective-permute-start(bf16[2,512,128]{2,1,0:T(8,128)(2,1)S(1)} %subtract_convert_fusion), channel_id=1, source_target_pairs={{0,32},{32,0},{64,96},{96,64},{128,160},{160,128},{192,224},{224,1... | collective-permute-start | bytes 786440 | tf_op jit(solution)/shard_map/ppermute | solution.py:55
  90.5 9.4 %all-to-all-done = f32[1,2,32,16,1,128]{5,3,1,4,0,2:T(8,128)S(1)} async-done(((f32[1,2,32,16,1,128]{5,3,1,4,0,2:T(8,128)}), f32[1,2,32,16,1,128]{5,3,1,4,0,2:T(8,128)S(1)}, u32[]{:S(2)}, u32[]{:S(2)}) %all-to-all-start) | async-done | bytes 524320 | tf_op jit(solution)/shard_map/all_to_all | solution.py:103
  100.5 2.3 %multiply_subtract_fusion = (f32[1,2,16,4096]{3,2,1,0:T(8,128)}, f32[1,2,16,4096]{3,2,1,0:T(8,128)}, f32[1,2,16,4096]{3,2,1,0:T(8,128)}) fusion(f32[1,2,16,4096]{3,2,1,0:T(8,128)S(1)} %copy-done.1, f32[]{:T(128)} %bitcast.29, f32[]{:T(128)} %bitcast.28, f32[]{:T(128)} %fusion.2, f32[1,2,16,4096]{3,0,2,1:T(1,128)S(1)} %bitcast.124, ...), kind=kLoop, calls=%fused_computation.13 | loop fusion | flops 1966080 | bytes 3670028 | tf_op jit(solution)/shard_map/sub | solution.py:74
  102.8 3.3 %collective-permute-start.16 = (bf16[2,512,128]{2,1,0:T(8,128)(2,1)S(1)}, bf16[2,512,128]{2,1,0:T(8,128)(2,1)S(1)}, u32[]{:S(2)}, u32[]{:S(2)}) collective-permute-start(bf16[2,512,128]{2,1,0:T(8,128)(2,1)S(1)} %get-tuple-element.31), channel_id=1, source_target_pairs={{0,192},{32,224},{64,0},{96,32},{128,64},{160,96},{192,128},{224,1... | collective-permute-start | bytes 786440 | tf_op jit(solution)/shard_map/ppermute | solution.py:64
  106.6 3.2 %collective-permute-done.15 = bf16[2,512,128]{2,1,0:T(8,128)(2,1)S(1)} collective-permute-done((bf16[2,512,128]{2,1,0:T(8,128)(2,1)S(1)}, bf16[2,512,128]{2,1,0:T(8,128)(2,1)S(1)}, u32[]{:S(2)}, u32[]{:S(2)}) %collective-permute-start.15) | collective-permute-done | bytes 262176 | tf_op jit(solution)/shard_map/ppermute | solution.py:63
  111.4 3.7 %collective-permute-start.18 = (bf16[2,512,128]{2,1,0:T(8,128)(2,1)S(1)}, bf16[2,512,128]{2,1,0:T(8,128)(2,1)S(1)}, u32[]{:S(2)}, u32[]{:S(2)}) collective-permute-start(bf16[2,512,128]{2,1,0:T(8,128)(2,1)S(1)} %collective-permute-done.16), channel_id=1, source_target_pairs={{0,192},{32,224},{64,0},{96,32},{128,64},{160,96},{192,128},{224,1... | collective-permute-start | bytes 786440 | tf_op jit(solution)/shard_map/ppermute | solution.py:64
  115.1 3.0 %collective-permute-done.17 = bf16[2,512,128]{2,1,0:T(8,128)(2,1)S(1)} collective-permute-done((bf16[2,512,128]{2,1,0:T(8,128)(2,1)S(1)}, bf16[2,512,128]{2,1,0:T(8,128)(2,1)S(1)}, u32[]{:S(2)}, u32[]{:S(2)}) %collective-permute-start.17) | collective-permute-done | bytes 262176 | tf_op jit(solution)/shard_map/ppermute | solution.py:63
  119.5 3.7 %collective-permute-start.20 = (bf16[2,512,128]{2,1,0:T(8,128)(2,1)S(1)}, bf16[2,512,128]{2,1,0:T(8,128)(2,1)S(1)}, u32[]{:S(2)}, u32[]{:S(2)}) collective-permute-start(bf16[2,512,128]{2,1,0:T(8,128)(2,1)S(1)} %collective-permute-done.18), channel_id=1, source_target_pairs={{0,192},{32,224},{64,0},{96,32},{128,64},{160,96},{192,128},{224,1... | collective-permute-start | bytes 786440 | tf_op jit(solution)/shard_map/ppermute | solution.py:64
  123.2 2.5 %collective-permute-done.19 = bf16[2,512,128]{2,1,0:T(8,128)(2,1)S(1)} collective-permute-done((bf16[2,512,128]{2,1,0:T(8,128)(2,1)S(1)}, bf16[2,512,128]{2,1,0:T(8,128)(2,1)S(1)}, u32[]{:S(2)}, u32[]{:S(2)}) %collective-permute-start.19) | collective-permute-done | bytes 262176 | tf_op jit(solution)/shard_map/ppermute | solution.py:63
  (80 shorter events, 28.9 us)
Async XLA Ops:
  5.2 9.6 %collective-permute-start = (f32[1,512,128]{2,1,0:T(8,128)}, f32[1,512,128]{2,1,0:T(8,128)}, u32[]{:S(2)}, u32[]{:S(2)}) collective-permute-start(f32[1,512,128]{2,1,0:T(8,128)} %get-tuple-element.18), channel_id=1, source_target_pairs={{0,64},{32,96},{64,128},{96,160},{128,192},{160,224},{192,0},{224,... | collective-permute-start | bytes 786440 | tf_op jit(solution)/shard_map/ppermute | solution.py:22
  6.8 8.1 %collective-permute-start.3 = (f32[1,512,128]{2,1,0:T(8,128)S(1)}, f32[1,512,128]{2,1,0:T(8,128)}, u32[]{:S(2)}, u32[]{:S(2)}) collective-permute-start(f32[1,512,128]{2,1,0:T(8,128)S(1)} %get-tuple-element.17), channel_id=1, source_target_pairs={{0,192},{32,224},{64,0},{96,32},{128,64},{160,96},{192,128},{224,1... | collective-permute-start | bytes 786440 | tf_op jit(solution)/shard_map/ppermute | solution.py:22
  10.8 37.0 %collective-permute-start.7 = (f32[1,4,512,128]{3,2,1,0:T(8,128)}, f32[1,4,512,128]{3,2,1,0:T(8,128)}, u32[]{:S(2)}, u32[]{:S(2)}) collective-permute-start(f32[1,4,512,128]{3,2,1,0:T(8,128)} %dynamic-slice_bitcast_fusion), channel_id=1, source_target_pairs={{0,32},{32,0},{64,96},{96,64},{128,160},{160,128},{192,224},{224,1... | collective-permute-start | bytes 3145736 | tf_op jit(solution)/shard_map/ppermute | solution.py:43
  16.7 15.6 %collective-permute-start.1 = (f32[1,512,128]{2,1,0:T(8,128)}, f32[1,512,128]{2,1,0:T(8,128)}, u32[]{:S(2)}, u32[]{:S(2)}) collective-permute-start(f32[1,512,128]{2,1,0:T(8,128)} %get-tuple-element.16), channel_id=1, source_target_pairs={{0,64},{32,96},{64,128},{96,160},{128,192},{160,224},{192,0},{224,... | collective-permute-start | bytes 786440 | tf_op jit(solution)/shard_map/ppermute | solution.py:22
  18.0 14.2 %collective-permute-start.4 = (f32[1,512,128]{2,1,0:T(8,128)S(1)}, f32[1,512,128]{2,1,0:T(8,128)}, u32[]{:S(2)}, u32[]{:S(2)}) collective-permute-start(f32[1,512,128]{2,1,0:T(8,128)S(1)} %get-tuple-element.15), channel_id=1, source_target_pairs={{0,192},{32,224},{64,0},{96,32},{128,64},{160,96},{192,128},{224,1... | collective-permute-start | bytes 786440 | tf_op jit(solution)/shard_map/ppermute | solution.py:22
  22.5 51.4 %all-to-all-start.1 = ((f32[3,1,2,1,16,32,128]{6,4,2,3,1,0,5:T(8,128)}), f32[3,1,2,1,16,32,128]{6,4,2,3,1,0,5:T(8,128)}, u32[]{:S(2)}, u32[]{:S(2)}) async-start(f32[3,1,2,1,16,32,128]{6,4,2,3,1,0,5:T(8,128)} %copy.52), calls=%async_computation.1 | async-start | bytes 3145728 | tf_op jit(solution)/shard_map/all_to_all | solution.py:94
  34.1 9.7 %collective-permute-start.2 = (f32[1,512,128]{2,1,0:T(8,128)}, f32[1,512,128]{2,1,0:T(8,128)S(1)}, u32[]{:S(2)}, u32[]{:S(2)}) collective-permute-start(f32[1,512,128]{2,1,0:T(8,128)} %get-tuple-element.14), channel_id=1, source_target_pairs={{0,64},{32,96},{64,128},{96,160},{128,192},{160,224},{192,0},{224,... | collective-permute-start | bytes 786440 | tf_op jit(solution)/shard_map/ppermute | solution.py:22
  34.3 9.6 %collective-permute-start.5 = (f32[1,512,128]{2,1,0:T(8,128)}, f32[1,512,128]{2,1,0:T(8,128)}, u32[]{:S(2)}, u32[]{:S(2)}) collective-permute-start(f32[1,512,128]{2,1,0:T(8,128)} %get-tuple-element.13), channel_id=1, source_target_pairs={{0,192},{32,224},{64,0},{96,32},{128,64},{160,96},{192,128},{224,1... | collective-permute-start | bytes 786440 | tf_op jit(solution)/shard_map/ppermute | solution.py:22
  45.0 14.1 %collective-permute-start.6 = (f32[1,512,128]{2,1,0:T(8,128)S(1)}, f32[1,512,128]{2,1,0:T(8,128)S(1)}, u32[]{:S(2)}, u32[]{:S(2)}) collective-permute-start(f32[1,512,128]{2,1,0:T(8,128)S(1)} %broadcast_select_fusion.2), channel_id=1, source_target_pairs={{0,32},{32,0},{64,96},{96,64},{128,160},{160,128},{192,224},{224,1... | collective-permute-start | bytes 786440 | tf_op jit(solution)/shard_map/ppermute | solution.py:39
  49.7 10.5 %collective-permute-start.8 = (f32[1,256,128]{2,1,0:T(8,128)S(1)}, f32[1,256,128]{2,1,0:T(8,128)S(1)}, u32[]{:S(2)}, u32[]{:S(2)}) collective-permute-start(f32[1,256,128]{2,1,0:T(8,128)S(1)} %slice.60), channel_id=1, source_target_pairs={{0,64},{32,96},{64,128},{96,160},{128,192},{160,224},{192,0},{224,... | collective-permute-start | bytes 393224 | tf_op jit(solution)/shard_map/ppermute | solution.py:22
  49.8 10.6 %collective-permute-start.11 = (f32[1,256,128]{2,1,0:T(8,128)S(1)}, f32[1,256,128]{2,1,0:T(8,128)S(1)}, u32[]{:S(2)}, u32[]{:S(2)}) collective-permute-start(f32[1,256,128]{2,1,0:T(8,128)S(1)} %slice.64), channel_id=1, source_target_pairs={{0,192},{32,224},{64,0},{96,32},{128,64},{160,96},{192,128},{224,1... | collective-permute-start | bytes 393224 | tf_op jit(solution)/shard_map/ppermute | solution.py:22
  60.2 6.3 %collective-permute-start.9 = (f32[1,256,128]{2,1,0:T(8,128)S(1)}, f32[1,256,128]{2,1,0:T(8,128)S(1)}, u32[]{:S(2)}, u32[]{:S(2)}) collective-permute-start(f32[1,256,128]{2,1,0:T(8,128)S(1)} %slice_add_fusion.5), channel_id=1, source_target_pairs={{0,64},{32,96},{64,128},{96,160},{128,192},{160,224},{192,0},{224,... | collective-permute-start | bytes 393224 | tf_op jit(solution)/shard_map/ppermute | solution.py:22
  60.4 6.4 %collective-permute-start.12 = (f32[1,256,128]{2,1,0:T(8,128)S(1)}, f32[1,256,128]{2,1,0:T(8,128)S(1)}, u32[]{:S(2)}, u32[]{:S(2)}) collective-permute-start(f32[1,256,128]{2,1,0:T(8,128)S(1)} %slice_add_fusion.2), channel_id=1, source_target_pairs={{0,192},{32,224},{64,0},{96,32},{128,64},{160,96},{192,128},{224,1... | collective-permute-start | bytes 393224 | tf_op jit(solution)/shard_map/ppermute | solution.py:22
  66.5 17.0 %copy-start.8 = (f32[64]{0:T(128)S(1)}, f32[64]{0:T(128)}, u32[]{:S(2)}) copy-start(f32[64]{0:T(128)} %param.12) | copy-start | bytes 772
  66.5 6.4 %collective-permute-start.10 = (f32[1,256,128]{2,1,0:T(8,128)S(1)}, f32[1,256,128]{2,1,0:T(8,128)S(1)}, u32[]{:S(2)}, u32[]{:S(2)}) collective-permute-start(f32[1,256,128]{2,1,0:T(8,128)S(1)} %slice_add_fusion.4), channel_id=1, source_target_pairs={{0,64},{32,96},{64,128},{96,160},{128,192},{160,224},{192,0},{224,... | collective-permute-start | bytes 393224 | tf_op jit(solution)/shard_map/ppermute | solution.py:22
  66.8 6.2 %collective-permute-start.13 = (f32[1,256,128]{2,1,0:T(8,128)S(1)}, f32[1,256,128]{2,1,0:T(8,128)S(1)}, u32[]{:S(2)}, u32[]{:S(2)}) collective-permute-start(f32[1,256,128]{2,1,0:T(8,128)S(1)} %slice_add_fusion.1), channel_id=1, source_target_pairs={{0,192},{32,224},{64,0},{96,32},{128,64},{160,96},{192,128},{224,1... | collective-permute-start | bytes 393224 | tf_op jit(solution)/shard_map/ppermute | solution.py:22
  73.9 26.0 %all-to-all-start = ((f32[1,2,32,16,1,128]{5,3,1,4,0,2:T(8,128)}), f32[1,2,32,16,1,128]{5,3,1,4,0,2:T(8,128)S(1)}, u32[]{:S(2)}, u32[]{:S(2)}) async-start(f32[1,2,32,16,1,128]{5,3,1,4,0,2:T(8,128)} %maximum_multiply_fusion), calls=%async_computation | async-start | bytes 1048576 | tf_op jit(solution)/shard_map/all_to_all | solution.py:103
  87.7 12.6 %collective-permute-start.14 = (bf16[2,512,128]{2,1,0:T(8,128)(2,1)S(1)}, bf16[2,512,128]{2,1,0:T(8,128)(2,1)S(1)}, u32[]{:S(2)}, u32[]{:S(2)}) collective-permute-start(bf16[2,512,128]{2,1,0:T(8,128)(2,1)S(1)} %subtract_convert_fusion), channel_id=1, source_target_pairs={{0,32},{32,0},{64,96},{96,64},{128,160},{160,128},{192,224},{224,1... | collective-permute-start | bytes 786440 | tf_op jit(solution)/shard_map/ppermute | solution.py:55
  100.4 9.4 %collective-permute-start.15 = (bf16[2,512,128]{2,1,0:T(8,128)(2,1)S(1)}, bf16[2,512,128]{2,1,0:T(8,128)(2,1)S(1)}, u32[]{:S(2)}, u32[]{:S(2)}) collective-permute-start(bf16[2,512,128]{2,1,0:T(8,128)(2,1)S(1)} %get-tuple-element.30), channel_id=1, source_target_pairs={{0,64},{32,96},{64,128},{96,160},{128,192},{160,224},{192,0},{224,... | collective-permute-start | bytes 786440 | tf_op jit(solution)/shard_map/ppermute | solution.py:63
  102.8 8.6 %collective-permute-start.16 = (bf16[2,512,128]{2,1,0:T(8,128)(2,1)S(1)}, bf16[2,512,128]{2,1,0:T(8,128)(2,1)S(1)}, u32[]{:S(2)}, u32[]{:S(2)}) collective-permute-start(bf16[2,512,128]{2,1,0:T(8,128)(2,1)S(1)} %get-tuple-element.31), channel_id=1, source_target_pairs={{0,192},{32,224},{64,0},{96,32},{128,64},{160,96},{192,128},{224,1... | collective-permute-start | bytes 786440 | tf_op jit(solution)/shard_map/ppermute | solution.py:64
  109.8 8.4 %collective-permute-start.17 = (bf16[2,512,128]{2,1,0:T(8,128)(2,1)S(1)}, bf16[2,512,128]{2,1,0:T(8,128)(2,1)S(1)}, u32[]{:S(2)}, u32[]{:S(2)}) collective-permute-start(bf16[2,512,128]{2,1,0:T(8,128)(2,1)S(1)} %collective-permute-done.15), channel_id=1, source_target_pairs={{0,64},{32,96},{64,128},{96,160},{128,192},{160,224},{192,0},{224,... | collective-permute-start | bytes 786440 | tf_op jit(solution)/shard_map/ppermute | solution.py:63
  111.4 8.1 %collective-permute-start.18 = (bf16[2,512,128]{2,1,0:T(8,128)(2,1)S(1)}, bf16[2,512,128]{2,1,0:T(8,128)(2,1)S(1)}, u32[]{:S(2)}, u32[]{:S(2)}) collective-permute-start(bf16[2,512,128]{2,1,0:T(8,128)(2,1)S(1)} %collective-permute-done.16), channel_id=1, source_target_pairs={{0,192},{32,224},{64,0},{96,32},{128,64},{160,96},{192,128},{224,1... | collective-permute-start | bytes 786440 | tf_op jit(solution)/shard_map/ppermute | solution.py:64
  118.1 7.6 %collective-permute-start.19 = (bf16[2,512,128]{2,1,0:T(8,128)(2,1)S(1)}, bf16[2,512,128]{2,1,0:T(8,128)(2,1)S(1)}, u32[]{:S(2)}, u32[]{:S(2)}) collective-permute-start(bf16[2,512,128]{2,1,0:T(8,128)(2,1)S(1)} %collective-permute-done.17), channel_id=1, source_target_pairs={{0,64},{32,96},{64,128},{96,160},{128,192},{160,224},{192,0},{224,... | collective-permute-start | bytes 786440 | tf_op jit(solution)/shard_map/ppermute | solution.py:63
  119.5 7.6 %collective-permute-start.20 = (bf16[2,512,128]{2,1,0:T(8,128)(2,1)S(1)}, bf16[2,512,128]{2,1,0:T(8,128)(2,1)S(1)}, u32[]{:S(2)}, u32[]{:S(2)}) collective-permute-start(bf16[2,512,128]{2,1,0:T(8,128)(2,1)S(1)} %collective-permute-done.18), channel_id=1, source_target_pairs={{0,192},{32,224},{64,0},{96,32},{128,64},{160,96},{192,128},{224,1... | collective-permute-start | bytes 786440 | tf_op jit(solution)/shard_map/ppermute | solution.py:64
  (8 other events, 62.4 us)

commit v3 on v1

--- a/solution.py
+++ b/solution.py
@@ -38,18 +38,24 @@
     d = lax.axis_index("dp")
     y = d // 2
     h = d % 2
+    lead, block, cols = mine.shape
+    rows = block // 2
+    out = jnp.zeros((lead, ring, 2, block, cols), mine.dtype)
+
+    def ring_along_y(piece, side):
+        nonlocal out
+        out = lax.dynamic_update_slice(out, piece[:, None, None], (0, y, side, 0, 0))
+        top = piece[:, :rows]
+        bottom = piece[:, rows:]
+        for t in range(ring - 1):
+            top = lax.ppermute(top, "dp", plus)
+            bottom = lax.ppermute(bottom, "dp", minus)
+            out = lax.dynamic_update_slice(out, top[:, None, None], (0, (y - t - 1) % ring, side, 0, 0))
+            out = lax.dynamic_update_slice(out, bottom[:, None, None], (0, (y + t + 1) % ring, side, rows, 0))
+
     other = lax.ppermute(mine, "dp", partner)
-    even = lax.select(h == 0, mine, other)
-    odd = lax.select(h == 0, other, mine)
-    lead, block, cols = mine.shape
-    out = jnp.zeros((lead, ring, 2, block, cols), mine.dtype)
-    out = lax.dynamic_update_slice(out, jnp.stack([even, odd], axis=1)[:, None], (0, y, 0, 0, 0))
-    up, down = even, odd
-    for t in range(ring - 1):
-        up = lax.ppermute(up, "dp", plus)
-        down = lax.ppermute(down, "dp", minus)
-        out = lax.dynamic_update_slice(out, up[:, None, None], (0, (y - t - 1) % ring, 0, 0, 0))
-        out = lax.dynamic_update_slice(out, down[:, None, None], (0, (y + t + 1) % ring, 1, 0, 0))
+    ring_along_y(mine, h)
+    ring_along_y(other, 1 - h)
     return out.reshape(lead, groups * block, cols)
 
 

time: 128 us -> 131 us (1.023)
  starting transfers between devices: 43.3 us -> 46.6 us
  waiting for transfers between devices: 53 us -> 56.1 us
  other arithmetic: 14.7 us -> 12.6 us
  local copies, waits for them, and re-layouts: 13.9 us -> 12.3 us
    ppermute x3, waiting for transfers between devices: 0.13 us -> 32.4 us  [_reduce_scatter_dp(): down = lax.ppermute(down, 'dp', minus)]
    ppermute x3, waiting for transfers between devices: 33.3 us -> 6.19 us  [_reduce_scatter_dp(): up = lax.ppermute(up, 'dp', plus)]
    ppermute x6 -> x12, starting transfers between devices: 9.95 us -> 16.5 us  [the longest x6 15.2 us: ring_along_y(): bottom = lax.ppermute(bottom, 'dp', minus)]
    ppermute x1, waiting for transfers between devices: 5.15 us -> 0.01 us  [_all_gather_dp(): other = lax.ppermute(mine, 'dp', partner)]
    ppermute x6 -> x12, waiting for transfers between devices: 4.64 us -> 9.78 us  [the longest x6 9.76 us: ring_along_y(): top = lax.ppermute(top, 'dp', plus)]
    convert_element_type x1 -> x0, other arithmetic: 2.4 us -> none  [_step(): fresh = fresh.astype(jnp.bfloat16).reshape(lead, block, panel_cols)]
    all_to_all x1, waiting for transfers between devices: 1.83 us -> 0.01 us  [_step(): lax.all_to_all(moved, 'shard', split_axis=2, concat_axis=4, tiled=True)]
    dynamic_update_slice x7 -> x14, local copies, waits for them, and re-layouts: 5.12 us -> 3.32 us  [the longest x6 1.7 us: ring_along_y(): lax.dynamic_update_slice(out, bottom[:, None, None], (0, (y + t + 1) % ri...]
  transfers between devices with their start and end apart: 16 -> 22, of which waited for: 8 -> 9; matrix products, arithmetic and copies ran while one was open for 15% -> 9% of each run, Pallas kernels for 0% -> 0%
where the time goes in v3:
time: 131 us; the launch traced here: 130 us
  waiting for transfers between devices  56.1 us (43%)
  starting transfers between devices  46.6 us (36%)
  other arithmetic  12.6 us (10%)
  local copies, waits for them, and re-layouts  12.3 us (9%)
  between operations  2.34 us (2%)
    ppermute x3, waiting for transfers between devices, _reduce_scatter_dp(): down = lax.ppermute(down, 'dp', minus)  32.4 us
    ppermute x6, starting transfers between devices, ring_along_y(): bottom = lax.ppermute(bottom, 'dp', minus)  15.2 us
    ppermute x6, waiting for transfers between devices, ring_along_y(): top = lax.ppermute(top, 'dp', plus)  9.76 us
    all_to_all x1, starting transfers between devices, _step(): lax.all_to_all(state, 'shard', split_axis=5, concat_axis=3, tiled=True)  9.65 us
    ppermute x1, waiting for transfers between devices, _reduce_scatter_dp(): return keep + lax.ppermute(send, 'dp', partner)  7.76 us
    all_to_all x1, starting transfers between devices, _step(): lax.all_to_all(moved, 'shard', split_axis=2, concat_axis=4, tiled=True)  7.72 us
    ppermute x3, waiting for transfers between devices, _reduce_scatter_dp(): up = lax.ppermute(up, 'dp', plus)  6.19 us
    unnamed x13, local copies, waits for them, and re-layouts  3.87 us
  transfers between devices with their start and end apart: 22, of which 9 were waited for; matrix products, arithmetic and copies ran while one was open for 9% of the time, Pallas kernels for 0%

profile of v3, /device:TPU:32, one launch (start us, length us, event | category | flops | bytes accessed | tf_op | source)
XLA Modules:
  0.0 130.0 jit_solution(6802010572788966387)
XLA Ops:
  3.3 2.1 %copy.78 = f32[3,1,2,1,16,32,128]{6,4,2,3,1,0,5:T(8,128)} copy(f32[3,1,2,1,16,32,128]{6,5,0,4,2,3,1:T(8,128)S(1)} %pad_maximum_fusion) | data formatting | bytes 3145728 | tf_op jit(solution)/shard_map/stack | solution.py:85
  5.3 9.7 %all-to-all-start.1 = ((f32[3,1,2,1,16,32,128]{6,4,2,3,1,0,5:T(8,128)}), f32[3,1,2,1,16,32,128]{6,4,2,3,1,0,5:T(8,128)S(1)}, u32[]{:S(2)}, u32[]{:S(2)}) async-start(f32[3,1,2,1,16,32,128]{6,4,2,3,1,0,5:T(8,128)} %copy.78), calls=%async_computation.1 | async-start | bytes 3145728 | tf_op jit(solution)/shard_map/all_to_all | solution.py:86
  16.3 3.1 %collective-permute-start.3 = (f32[2,512,128]{2,1,0:T(8,128)S(1)}, f32[2,512,128]{2,1,0:T(8,128)S(1)}, u32[]{:S(2)}, u32[]{:S(2)}) collective-permute-start(f32[2,512,128]{2,1,0:T(8,128)S(1)} %get-tuple-element.18), channel_id=1, source_target_pairs={{0,192},{32,224},{64,0},{96,32},{128,64},{160,96},{192,128},{224,1... | collective-permute-start | bytes 1572872 | tf_op jit(solution)/shard_map/ppermute | solution.py:28
  19.4 11.5 %collective-permute-done.3 = f32[2,512,128]{2,1,0:T(8,128)S(1)} collective-permute-done((f32[2,512,128]{2,1,0:T(8,128)S(1)}, f32[2,512,128]{2,1,0:T(8,128)S(1)}, u32[]{:S(2)}, u32[]{:S(2)}) %collective-permute-start.3) | collective-permute-done | bytes 524320 | tf_op jit(solution)/shard_map/ppermute | solution.py:28
  30.9 3.5 %collective-permute-done = f32[2,512,128]{2,1,0:T(8,128)} collective-permute-done((f32[2,512,128]{2,1,0:T(8,128)S(1)}, f32[2,512,128]{2,1,0:T(8,128)}, u32[]{:S(2)}, u32[]{:S(2)}) %collective-permute-start) | collective-permute-done | bytes 524320 | tf_op jit(solution)/shard_map/ppermute | solution.py:27
  36.1 1.8 %collective-permute-start.1 = (f32[2,512,128]{2,1,0:T(8,128)S(1)}, f32[2,512,128]{2,1,0:T(8,128)}, u32[]{:S(2)}, u32[]{:S(2)}) collective-permute-start(f32[2,512,128]{2,1,0:T(8,128)S(1)} %get-tuple-element.17), channel_id=1, source_target_pairs={{0,64},{32,96},{64,128},{96,160},{128,192},{160,224},{192,0},{224,... | collective-permute-start | bytes 1572872 | tf_op jit(solution)/shard_map/ppermute | solution.py:27
  38.0 10.8 %collective-permute-done.4 = f32[2,512,128]{2,1,0:T(8,128)S(1)} collective-permute-done((f32[2,512,128]{2,1,0:T(8,128)S(1)}, f32[2,512,128]{2,1,0:T(8,128)S(1)}, u32[]{:S(2)}, u32[]{:S(2)}) %collective-permute-start.4) | collective-permute-done | bytes 524320 | tf_op jit(solution)/shard_map/ppermute | solution.py:28
  50.3 2.3 %bitcast_add_fusion.1 = (f32[2,512,128]{2,1,0:T(8,128)}, f32[2,512,128]{2,1,0:T(8,128)S(1)}) fusion(f32[2,512,128]{2,1,0:T(8,128)S(1)} %collective-permute-done.4, f32[2,8,512,128]{3,2,1,0:T(8,128)} %bitcast.112, s32[]{:T(128)S(6)} %select_n.167, f32[2,512,128]{2,1,0:T(8,128)} %collective-permute-done.1, s32[]{:T(128)S(6)} %select_n.159), kind=kLoop, calls=%fused_computation.7 | loop fusion | flops 262144 | bytes 3145736 | tf_op jit(solution)/shard_map/add | solution.py:30
  52.7 1.8 %collective-permute-start.2 = (f32[2,512,128]{2,1,0:T(8,128)S(1)}, f32[2,512,128]{2,1,0:T(8,128)S(1)}, u32[]{:S(2)}, u32[]{:S(2)}) collective-permute-start(f32[2,512,128]{2,1,0:T(8,128)S(1)} %get-tuple-element.15), channel_id=1, source_target_pairs={{0,64},{32,96},{64,128},{96,160},{128,192},{160,224},{192,0},{224,... | collective-permute-start | bytes 1572872 | tf_op jit(solution)/shard_map/ppermute | solution.py:27
  54.5 10.1 %collective-permute-done.5 = f32[2,512,128]{2,1,0:T(8,128)S(1)} collective-permute-done((f32[2,512,128]{2,1,0:T(8,128)}, f32[2,512,128]{2,1,0:T(8,128)S(1)}, u32[]{:S(2)}, u32[]{:S(2)}) %collective-permute-start.5) | collective-permute-done | bytes 524320 | tf_op jit(solution)/shard_map/ppermute | solution.py:28
  65.9 2.1 %broadcast_select_fusion = f32[2,512,128]{2,1,0:T(8,128)} fusion(pred[]{:T(512)S(6)} %eq.41, f32[2,512,128]{2,1,0:T(8,128)S(1)} %collective-permute-done.2, f32[2,8,512,128]{3,2,1,0:T(8,128)} %bitcast.113, s32[]{:T(128)S(6)} %select_n.161, f32[2,512,128]{2,1,0:T(8,128)S(1)} %collective-permute-done.5, s32[]{:T(128)S(6)} %select_n.169), kind=kLoop, calls=%fused_computation.21 | loop fusion | flops 393216 | bytes 2621449 | tf_op jit(solution)/shard_map/select_n | solution.py:32
  67.9 2.7 %collective-permute-start.6 = (f32[2,512,128]{2,1,0:T(8,128)}, f32[2,512,128]{2,1,0:T(8,128)S(1)}, u32[]{:S(2)}, u32[]{:S(2)}) collective-permute-start(f32[2,512,128]{2,1,0:T(8,128)} %broadcast_select_fusion), channel_id=1, source_target_pairs={{0,32},{32,0},{64,96},{96,64},{128,160},{160,128},{192,224},{224,1... | collective-permute-start | bytes 1572872 | tf_op jit(solution)/shard_map/ppermute | solution.py:33
  73.0 7.8 %collective-permute-done.6 = f32[2,512,128]{2,1,0:T(8,128)S(1)} collective-permute-done((f32[2,512,128]{2,1,0:T(8,128)}, f32[2,512,128]{2,1,0:T(8,128)S(1)}, u32[]{:S(2)}, u32[]{:S(2)}) %collective-permute-start.6) | collective-permute-done | bytes 524320 | tf_op jit(solution)/shard_map/ppermute | solution.py:33
  82.6 2.4 %bitcast_dynamic-update-slice_fusion.1 = (bf16[2,4,2,512,128]{4,3,0,2,1:T(8,128)(2,1)S(1)}, bf16[2,512,128]{2,1,0:T(8,128)(2,1)S(1)}, f32[2,512,128]{2,1,0:T(8,128)S(1)}) fusion(bf16[2,4,2,512,128]{4,3,0,2,1:T(8,128)(2,1)S(1)} %broadcast_in_dim.46, s32[]{:T(128)S(6)} %select_n.172, s32[]{:T(128)S(6)} %select_n.173, f32[2,512,128]{2,1,0:T(8,128)S(1)} %bitcast.118, ...), kind=kLoop, calls=%fused_computation.19 | loop fusion | flops 2490368 | bytes 5242909 | tf_op jit(solution)/shard_map/dynamic_update_slice | solution.py:47
  85.0 2.8 %collective-permute-start.13 = (bf16[2,512,128]{2,1,0:T(8,128)(2,1)S(1)}, bf16[2,512,128]{2,1,0:T(8,128)(2,1)S(1)}, u32[]{:S(2)}, u32[]{:S(2)}) collective-permute-start(bf16[2,512,128]{2,1,0:T(8,128)(2,1)S(1)} %get-tuple-element.9), channel_id=1, source_target_pairs={{0,32},{32,0},{64,96},{96,64},{128,160},{160,128},{192,224},{224,1... | collective-permute-start | bytes 786440 | tf_op jit(solution)/shard_map/ppermute | solution.py:56
  90.7 7.7 %all-to-all-start = ((f32[1,2,32,16,1,128]{5,3,1,4,0,2:T(8,128)}), f32[1,2,32,16,1,128]{5,3,1,4,0,2:T(8,128)S(1)}, u32[]{:S(2)}, u32[]{:S(2)}) async-start(f32[1,2,32,16,1,128]{5,3,1,4,0,2:T(8,128)} %copy.73), calls=%async_computation | async-start | bytes 1048576 | tf_op jit(solution)/shard_map/all_to_all | solution.py:95
  98.5 2.2 %collective-permute-start.10 = (bf16[2,256,128]{2,1,0:T(8,128)(2,1)}, bf16[2,256,128]{2,1,0:T(8,128)(2,1)S(1)}, u32[]{:S(2)}, u32[]{:S(2)}) collective-permute-start(bf16[2,256,128]{2,1,0:T(8,128)(2,1)} %collective-permute-done.8), channel_id=1, source_target_pairs={{0,192},{32,224},{64,0},{96,32},{128,64},{160,96},{192,128},{224,1... | collective-permute-start | bytes 393224 | tf_op jit(solution)/shard_map/ppermute | solution.py:52
  101.7 3.3 %collective-permute-start.15 = (bf16[2,256,128]{2,1,0:T(8,128)(2,1)S(1)}, bf16[2,256,128]{2,1,0:T(8,128)(2,1)S(1)}, u32[]{:S(2)}, u32[]{:S(2)}) collective-permute-start(bf16[2,256,128]{2,1,0:T(8,128)(2,1)S(1)} %get-tuple-element.23), channel_id=1, source_target_pairs={{0,192},{32,224},{64,0},{96,32},{128,64},{160,96},{192,128},{224,1... | collective-permute-start | bytes 393224 | tf_op jit(solution)/shard_map/ppermute | solution.py:52
  105.0 3.2 %collective-permute-start.12 = (bf16[2,256,128]{2,1,0:T(8,128)(2,1)S(1)}, bf16[2,256,128]{2,1,0:T(8,128)(2,1)S(1)}, u32[]{:S(2)}, u32[]{:S(2)}) collective-permute-start(bf16[2,256,128]{2,1,0:T(8,128)(2,1)S(1)} %collective-permute-done.10), channel_id=1, source_target_pairs={{0,192},{32,224},{64,0},{96,32},{128,64},{160,96},{192,128},{224,1... | collective-permute-start | bytes 393224 | tf_op jit(solution)/shard_map/ppermute | solution.py:52
  108.3 3.3 %collective-permute-start.17 = (bf16[2,256,128]{2,1,0:T(8,128)(2,1)S(1)}, bf16[2,256,128]{2,1,0:T(8,128)(2,1)S(1)}, u32[]{:S(2)}, u32[]{:S(2)}) collective-permute-start(bf16[2,256,128]{2,1,0:T(8,128)(2,1)S(1)} %collective-permute-done.15), channel_id=1, source_target_pairs={{0,192},{32,224},{64,0},{96,32},{128,64},{160,96},{192,128},{224,1... | collective-permute-start | bytes 393224 | tf_op jit(solution)/shard_map/ppermute | solution.py:52
  111.6 3.6 %collective-permute-done.11 = bf16[2,256,128]{2,1,0:T(8,128)(2,1)S(1)} collective-permute-done((bf16[2,256,128]{2,1,0:T(8,128)(2,1)S(1)}, bf16[2,256,128]{2,1,0:T(8,128)(2,1)S(1)}, u32[]{:S(2)}, u32[]{:S(2)}) %collective-permute-start.11) | collective-permute-done | bytes 131104 | tf_op jit(solution)/shard_map/ppermute | solution.py:51
  115.5 2.4 %collective-permute-start.19 = (bf16[2,256,128]{2,1,0:T(8,128)(2,1)S(1)}, bf16[2,256,128]{2,1,0:T(8,128)(2,1)S(1)}, u32[]{:S(2)}, u32[]{:S(2)}) collective-permute-start(bf16[2,256,128]{2,1,0:T(8,128)(2,1)S(1)} %collective-permute-done.17), channel_id=1, source_target_pairs={{0,192},{32,224},{64,0},{96,32},{128,64},{160,96},{192,128},{224,1... | collective-permute-start | bytes 393224 | tf_op jit(solution)/shard_map/ppermute | solution.py:52
  117.9 6.1 %collective-permute-done.18 = bf16[2,256,128]{2,1,0:T(8,128)(2,1)S(1)} collective-permute-done((bf16[2,256,128]{2,1,0:T(8,128)(2,1)S(1)}, bf16[2,256,128]{2,1,0:T(8,128)(2,1)S(1)}, u32[]{:S(2)}, u32[]{:S(2)}) %collective-permute-start.18) | collective-permute-done | bytes 131104 | tf_op jit(solution)/shard_map/ppermute | solution.py:51
  126.5 3.5 %multiply_subtract_fusion = (f32[1,2,16,4096]{3,2,1,0:T(8,128)}, f32[1,2,16,4096]{3,2,1,0:T(8,128)}, f32[1,2,16,4096]{3,2,1,0:T(8,128)}) fusion(f32[1,2,16,4096]{3,2,1,0:T(8,128)S(1)} %copy-done.1, f32[]{:T(128)} %bitcast.15, f32[]{:T(128)} %bitcast.14, f32[]{:T(128)} %fusion.1, f32[1,2,16,4096]{3,0,2,1:T(1,128)S(1)} %bitcast.123, ...), kind=kLoop, calls=%fused_computation.13 | loop fusion | flops 1966080 | bytes 3670028 | tf_op jit(solution)/shard_map/sub | solution.py:66
  (64 shorter events, 17.8 us)
Async XLA Ops:
  5.3 67.4 %all-to-all-start.1 = ((f32[3,1,2,1,16,32,128]{6,4,2,3,1,0,5:T(8,128)}), f32[3,1,2,1,16,32,128]{6,4,2,3,1,0,5:T(8,128)S(1)}, u32[]{:S(2)}, u32[]{:S(2)}) async-start(f32[3,1,2,1,16,32,128]{6,4,2,3,1,0,5:T(8,128)} %copy.78), calls=%async_computation.1 | async-start | bytes 3145728 | tf_op jit(solution)/shard_map/all_to_all | solution.py:86
  16.3 14.6 %collective-permute-start.3 = (f32[2,512,128]{2,1,0:T(8,128)S(1)}, f32[2,512,128]{2,1,0:T(8,128)S(1)}, u32[]{:S(2)}, u32[]{:S(2)}) collective-permute-start(f32[2,512,128]{2,1,0:T(8,128)S(1)} %get-tuple-element.18), channel_id=1, source_target_pairs={{0,192},{32,224},{64,0},{96,32},{128,64},{160,96},{192,128},{224,1... | collective-permute-start | bytes 1572872 | tf_op jit(solution)/shard_map/ppermute | solution.py:28
  19.4 15.0 %collective-permute-start = (f32[2,512,128]{2,1,0:T(8,128)S(1)}, f32[2,512,128]{2,1,0:T(8,128)}, u32[]{:S(2)}, u32[]{:S(2)}) collective-permute-start(f32[2,512,128]{2,1,0:T(8,128)S(1)} %get-tuple-element.19), channel_id=1, source_target_pairs={{0,64},{32,96},{64,128},{96,160},{128,192},{160,224},{192,0},{224,... | collective-permute-start | bytes 1572872 | tf_op jit(solution)/shard_map/ppermute | solution.py:27
  35.9 12.9 %collective-permute-start.4 = (f32[2,512,128]{2,1,0:T(8,128)S(1)}, f32[2,512,128]{2,1,0:T(8,128)S(1)}, u32[]{:S(2)}, u32[]{:S(2)}) collective-permute-start(f32[2,512,128]{2,1,0:T(8,128)S(1)} %get-tuple-element.16), channel_id=1, source_target_pairs={{0,192},{32,224},{64,0},{96,32},{128,64},{160,96},{192,128},{224,1... | collective-permute-start | bytes 1572872 | tf_op jit(solution)/shard_map/ppermute | solution.py:28
  36.1 14.1 %collective-permute-start.1 = (f32[2,512,128]{2,1,0:T(8,128)S(1)}, f32[2,512,128]{2,1,0:T(8,128)}, u32[]{:S(2)}, u32[]{:S(2)}) collective-permute-start(f32[2,512,128]{2,1,0:T(8,128)S(1)} %get-tuple-element.17), channel_id=1, source_target_pairs={{0,64},{32,96},{64,128},{96,160},{128,192},{160,224},{192,0},{224,... | collective-permute-start | bytes 1572872 | tf_op jit(solution)/shard_map/ppermute | solution.py:27
  52.5 19.6 %copy-start.4 = (f32[64]{0:T(128)S(1)}, f32[64]{0:T(128)}, u32[]{:S(2)}) copy-start(f32[64]{0:T(128)} %param.12) | copy-start | bytes 772
  52.5 12.2 %collective-permute-start.5 = (f32[2,512,128]{2,1,0:T(8,128)}, f32[2,512,128]{2,1,0:T(8,128)S(1)}, u32[]{:S(2)}, u32[]{:S(2)}) collective-permute-start(f32[2,512,128]{2,1,0:T(8,128)} %get-tuple-element.14), channel_id=1, source_target_pairs={{0,192},{32,224},{64,0},{96,32},{128,64},{160,96},{192,128},{224,1... | collective-permute-start | bytes 1572872 | tf_op jit(solution)/shard_map/ppermute | solution.py:28
  52.7 13.2 %collective-permute-start.2 = (f32[2,512,128]{2,1,0:T(8,128)S(1)}, f32[2,512,128]{2,1,0:T(8,128)S(1)}, u32[]{:S(2)}, u32[]{:S(2)}) collective-permute-start(f32[2,512,128]{2,1,0:T(8,128)S(1)} %get-tuple-element.15), channel_id=1, source_target_pairs={{0,64},{32,96},{64,128},{96,160},{128,192},{160,224},{192,0},{224,... | collective-permute-start | bytes 1572872 | tf_op jit(solution)/shard_map/ppermute | solution.py:27
  67.9 12.8 %collective-permute-start.6 = (f32[2,512,128]{2,1,0:T(8,128)}, f32[2,512,128]{2,1,0:T(8,128)S(1)}, u32[]{:S(2)}, u32[]{:S(2)}) collective-permute-start(f32[2,512,128]{2,1,0:T(8,128)} %broadcast_select_fusion), channel_id=1, source_target_pairs={{0,32},{32,0},{64,96},{96,64},{128,160},{160,128},{192,224},{224,1... | collective-permute-start | bytes 1572872 | tf_op jit(solution)/shard_map/ppermute | solution.py:33
  85.0 16.7 %collective-permute-start.13 = (bf16[2,512,128]{2,1,0:T(8,128)(2,1)S(1)}, bf16[2,512,128]{2,1,0:T(8,128)(2,1)S(1)}, u32[]{:S(2)}, u32[]{:S(2)}) collective-permute-start(bf16[2,512,128]{2,1,0:T(8,128)(2,1)S(1)} %get-tuple-element.9), channel_id=1, source_target_pairs={{0,32},{32,0},{64,96},{96,64},{128,160},{160,128},{192,224},{224,1... | collective-permute-start | bytes 786440 | tf_op jit(solution)/shard_map/ppermute | solution.py:56
  87.8 10.7 %collective-permute-start.8 = (bf16[2,256,128]{2,1,0:T(8,128)(2,1)S(1)}, bf16[2,256,128]{2,1,0:T(8,128)(2,1)}, u32[]{:S(2)}, u32[]{:S(2)}) collective-permute-start(bf16[2,256,128]{2,1,0:T(8,128)(2,1)S(1)} %get-tuple-element.25), channel_id=1, source_target_pairs={{0,192},{32,224},{64,0},{96,32},{128,64},{160,96},{192,128},{224,1... | collective-permute-start | bytes 393224 | tf_op jit(solution)/shard_map/ppermute | solution.py:52
  88.6 12.1 %collective-permute-start.7 = (bf16[2,256,128]{2,1,0:T(8,128)(2,1)S(1)}, bf16[2,256,128]{2,1,0:T(8,128)(2,1)S(1)}, u32[]{:S(2)}, u32[]{:S(2)}) collective-permute-start(bf16[2,256,128]{2,1,0:T(8,128)(2,1)S(1)} %get-tuple-element.26), channel_id=1, source_target_pairs={{0,64},{32,96},{64,128},{96,160},{128,192},{160,224},{192,0},{224,... | collective-permute-start | bytes 393224 | tf_op jit(solution)/shard_map/ppermute | solution.py:51
  90.7 35.4 %all-to-all-start = ((f32[1,2,32,16,1,128]{5,3,1,4,0,2:T(8,128)}), f32[1,2,32,16,1,128]{5,3,1,4,0,2:T(8,128)S(1)}, u32[]{:S(2)}, u32[]{:S(2)}) async-start(f32[1,2,32,16,1,128]{5,3,1,4,0,2:T(8,128)} %copy.73), calls=%async_computation | async-start | bytes 1048576 | tf_op jit(solution)/shard_map/all_to_all | solution.py:95
  98.5 6.6 %collective-permute-start.10 = (bf16[2,256,128]{2,1,0:T(8,128)(2,1)}, bf16[2,256,128]{2,1,0:T(8,128)(2,1)S(1)}, u32[]{:S(2)}, u32[]{:S(2)}) collective-permute-start(bf16[2,256,128]{2,1,0:T(8,128)(2,1)} %collective-permute-done.8), channel_id=1, source_target_pairs={{0,192},{32,224},{64,0},{96,32},{128,64},{160,96},{192,128},{224,1... | collective-permute-start | bytes 393224 | tf_op jit(solution)/shard_map/ppermute | solution.py:52
  100.7 7.5 %collective-permute-start.9 = (bf16[2,256,128]{2,1,0:T(8,128)(2,1)S(1)}, bf16[2,256,128]{2,1,0:T(8,128)(2,1)S(1)}, u32[]{:S(2)}, u32[]{:S(2)}) collective-permute-start(bf16[2,256,128]{2,1,0:T(8,128)(2,1)S(1)} %collective-permute-done.7), channel_id=1, source_target_pairs={{0,64},{32,96},{64,128},{96,160},{128,192},{160,224},{192,0},{224,... | collective-permute-start | bytes 393224 | tf_op jit(solution)/shard_map/ppermute | solution.py:51
  101.7 6.6 %collective-permute-start.15 = (bf16[2,256,128]{2,1,0:T(8,128)(2,1)S(1)}, bf16[2,256,128]{2,1,0:T(8,128)(2,1)S(1)}, u32[]{:S(2)}, u32[]{:S(2)}) collective-permute-start(bf16[2,256,128]{2,1,0:T(8,128)(2,1)S(1)} %get-tuple-element.23), channel_id=1, source_target_pairs={{0,192},{32,224},{64,0},{96,32},{128,64},{160,96},{192,128},{224,1... | collective-permute-start | bytes 393224 | tf_op jit(solution)/shard_map/ppermute | solution.py:52
  105.0 6.6 %collective-permute-start.14 = (bf16[2,256,128]{2,1,0:T(8,128)(2,1)S(1)}, bf16[2,256,128]{2,1,0:T(8,128)(2,1)S(1)}, u32[]{:S(2)}, u32[]{:S(2)}) collective-permute-start(bf16[2,256,128]{2,1,0:T(8,128)(2,1)S(1)} %get-tuple-element.24), channel_id=1, source_target_pairs={{0,64},{32,96},{64,128},{96,160},{128,192},{160,224},{192,0},{224,... | collective-permute-start | bytes 393224 | tf_op jit(solution)/shard_map/ppermute | solution.py:51
  105.0 10.3 %collective-permute-start.12 = (bf16[2,256,128]{2,1,0:T(8,128)(2,1)S(1)}, bf16[2,256,128]{2,1,0:T(8,128)(2,1)S(1)}, u32[]{:S(2)}, u32[]{:S(2)}) collective-permute-start(bf16[2,256,128]{2,1,0:T(8,128)(2,1)S(1)} %collective-permute-done.10), channel_id=1, source_target_pairs={{0,192},{32,224},{64,0},{96,32},{128,64},{160,96},{192,128},{224,1... | collective-permute-start | bytes 393224 | tf_op jit(solution)/shard_map/ppermute | solution.py:52
  108.3 7.0 %collective-permute-start.11 = (bf16[2,256,128]{2,1,0:T(8,128)(2,1)S(1)}, bf16[2,256,128]{2,1,0:T(8,128)(2,1)S(1)}, u32[]{:S(2)}, u32[]{:S(2)}) collective-permute-start(bf16[2,256,128]{2,1,0:T(8,128)(2,1)S(1)} %collective-permute-done.9), channel_id=1, source_target_pairs={{0,64},{32,96},{64,128},{96,160},{128,192},{160,224},{192,0},{224,... | collective-permute-start | bytes 393224 | tf_op jit(solution)/shard_map/ppermute | solution.py:51
  108.3 7.1 %collective-permute-start.17 = (bf16[2,256,128]{2,1,0:T(8,128)(2,1)S(1)}, bf16[2,256,128]{2,1,0:T(8,128)(2,1)S(1)}, u32[]{:S(2)}, u32[]{:S(2)}) collective-permute-start(bf16[2,256,128]{2,1,0:T(8,128)(2,1)S(1)} %collective-permute-done.15), channel_id=1, source_target_pairs={{0,192},{32,224},{64,0},{96,32},{128,64},{160,96},{192,128},{224,1... | collective-permute-start | bytes 393224 | tf_op jit(solution)/shard_map/ppermute | solution.py:52
  111.6 6.2 %collective-permute-start.16 = (bf16[2,256,128]{2,1,0:T(8,128)(2,1)S(1)}, bf16[2,256,128]{2,1,0:T(8,128)(2,1)S(1)}, u32[]{:S(2)}, u32[]{:S(2)}) collective-permute-start(bf16[2,256,128]{2,1,0:T(8,128)(2,1)S(1)} %collective-permute-done.14), channel_id=1, source_target_pairs={{0,64},{32,96},{64,128},{96,160},{128,192},{160,224},{192,0},{224,... | collective-permute-start | bytes 393224 | tf_op jit(solution)/shard_map/ppermute | solution.py:51
  115.5 10.0 %collective-permute-start.19 = (bf16[2,256,128]{2,1,0:T(8,128)(2,1)S(1)}, bf16[2,256,128]{2,1,0:T(8,128)(2,1)S(1)}, u32[]{:S(2)}, u32[]{:S(2)}) collective-permute-start(bf16[2,256,128]{2,1,0:T(8,128)(2,1)S(1)} %collective-permute-done.17), channel_id=1, source_target_pairs={{0,192},{32,224},{64,0},{96,32},{128,64},{160,96},{192,128},{224,1... | collective-permute-start | bytes 393224 | tf_op jit(solution)/shard_map/ppermute | solution.py:52
  117.8 6.2 %collective-permute-start.18 = (bf16[2,256,128]{2,1,0:T(8,128)(2,1)S(1)}, bf16[2,256,128]{2,1,0:T(8,128)(2,1)S(1)}, u32[]{:S(2)}, u32[]{:S(2)}) collective-permute-start(bf16[2,256,128]{2,1,0:T(8,128)(2,1)S(1)} %collective-permute-done.16), channel_id=1, source_target_pairs={{0,64},{32,96},{64,128},{96,160},{128,192},{160,224},{192,0},{224,... | collective-permute-start | bytes 393224 | tf_op jit(solution)/shard_map/ppermute | solution.py:51
  124.0 2.5 %copy-start.1 = (f32[1,2,16,4096]{3,2,1,0:T(8,128)S(1)}, f32[1,2,16,4096]{3,2,1,0:T(8,128)}, u32[]{:S(2)}) copy-start(f32[1,2,16,4096]{3,2,1,0:T(8,128)} %param.8) | copy-start | bytes 1572868
  (3 other events, 4.2 us)

commit v4 on v1

--- a/solution.py
+++ b/solution.py
@@ -21,16 +21,21 @@
     d = lax.axis_index("dp")
     y = d // 2
     h = d % 2
+    raw = lax.ppermute(_take(x, 2 * y + 1 - h), "dp", partner)
     up = _take(x, 2 * ((y - 1) % ring))
     down = _take(x, 2 * ((y + 1) % ring) + 1)
-    for t in range(ring - 1):
+    for t in range(ring - 2):
         up = lax.ppermute(up, "dp", plus)
         down = lax.ppermute(down, "dp", minus)
         up = up + _take(x, 2 * ((y - t - 2) % ring))
         down = down + _take(x, 2 * ((y + t + 2) % ring) + 1)
-    keep = lax.select(h == 0, up, down)
-    send = lax.select(h == 0, down, up)
-    return keep + lax.ppermute(send, "dp", partner)
+    within = [(2 * r, 2 * ((r + 1) % ring)) for r in range(ring)]
+    within += [(2 * r + 1, 2 * ((r - 1) % ring) + 1) for r in range(ring)]
+    across = [(2 * r + 1, 2 * ((r + 1) % ring)) for r in range(ring)]
+    across += [(2 * r, 2 * ((r - 1) % ring) + 1) for r in range(ring)]
+    same = lax.ppermute(lax.select(h == 0, up, down), "dp", within)
+    other = lax.ppermute(lax.select(h == 0, down, up), "dp", across)
+    return (_take(x, 2 * y + h) + same) + (other + raw)
 
 
 def _all_gather_dp(mine, groups):
@@ -38,16 +43,23 @@
     d = lax.axis_index("dp")
     y = d // 2
     h = d % 2
+    lead, block, cols = mine.shape
+    within = [(2 * r, 2 * ((r + 1) % ring)) for r in range(ring)]
+    within += [(2 * r + 1, 2 * ((r - 1) % ring) + 1) for r in range(ring)]
+    across = [(2 * r, 2 * ((r + 1) % ring) + 1) for r in range(ring)]
+    across += [(2 * r + 1, 2 * ((r - 1) % ring)) for r in range(ring)]
     other = lax.ppermute(mine, "dp", partner)
-    even = lax.select(h == 0, mine, other)
-    odd = lax.select(h == 0, other, mine)
-    lead, block, cols = mine.shape
+    same = lax.ppermute(mine, "dp", within)
+    diagonal = lax.ppermute(mine, "dp", across)
+    up = lax.select(h == 0, same, diagonal)
+    down = lax.select(h == 0, diagonal, same)
     out = jnp.zeros((lead, ring, 2, block, cols), mine.dtype)
-    out = lax.dynamic_update_slice(out, jnp.stack([even, odd], axis=1)[:, None], (0, y, 0, 0, 0))
-    up, down = even, odd
+    out = lax.dynamic_update_slice(out, mine[:, None, None], (0, y, h, 0, 0))
+    out = lax.dynamic_update_slice(out, other[:, None, None], (0, y, 1 - h, 0, 0))
     for t in range(ring - 1):
-        up = lax.ppermute(up, "dp", plus)
-        down = lax.ppermute(down, "dp", minus)
+        if t:
+            up = lax.ppermute(up, "dp", plus)
+            down = lax.ppermute(down, "dp", minus)
         out = lax.dynamic_update_slice(out, up[:, None, None], (0, (y - t - 1) % ring, 0, 0, 0))
         out = lax.dynamic_update_slice(out, down[:, None, None], (0, (y + t + 1) % ring, 1, 0, 0))
     return out.reshape(lead, groups * block, cols)

time: 128 us -> 135 us (1.055)
  waiting for transfers between devices: 53 us -> 61.7 us
  starting transfers between devices: 43.3 us -> 40.8 us
    ppermute x3 -> x2, waiting for transfers between devices: 33.3 us -> 4.91 us  [_reduce_scatter_dp(): up = lax.ppermute(up, 'dp', plus)]
    ppermute x3 -> x2, waiting for transfers between devices: 0.13 us -> 20.1 us  [_reduce_scatter_dp(): down = lax.ppermute(down, 'dp', minus)]
    ppermute x1 -> x5, waiting for transfers between devices: 7.91 us -> 19.6 us  [the longest x1 19.3 us: _reduce_scatter_dp(): same = lax.ppermute(lax.select(h == 0, up, down), 'dp', within)]
    ppermute x1 -> x5, starting transfers between devices: 2.73 us -> 9.3 us  [the longest x1 3.47 us: _all_gather_dp(): diagonal = lax.ppermute(mine, 'dp', across)]
    dynamic_update_slice x1 -> x3, other arithmetic: 1.08 us -> 5.99 us  [the longest x1 3.38 us: _all_gather_dp(): out = lax.dynamic_update_slice(out, mine[:, None, None], (0, y, h, 0, 0))]
    ppermute x3 -> x2, waiting for transfers between devices: 4.64 us -> 8.4 us  [_all_gather_dp(): up = lax.ppermute(up, 'dp', plus)]
    ppermute x3 -> x2, starting transfers between devices: 4.56 us -> 1.53 us  [_reduce_scatter_dp(): up = lax.ppermute(up, 'dp', plus)]
    convert_element_type x1 -> x0, other arithmetic: 2.4 us -> none  [_step(): fresh = fresh.astype(jnp.bfloat16).reshape(lead, block, panel_cols)]
  transfers between devices with their start and end apart: 16 -> 16, of which waited for: 8 -> 9; matrix products, arithmetic and copies ran while one was open for 15% -> 10% of each run, Pallas kernels for 0% -> 0%
where the time goes in v4:
time: 135 us; the launch traced here: 133 us
  waiting for transfers between devices  61.7 us (46%)
  starting transfers between devices  40.8 us (30%)
  other arithmetic  15.7 us (12%)
  local copies, waits for them, and re-layouts  12.7 us (9%)
  between operations  2.28 us (2%)
    ppermute x2, waiting for transfers between devices, _reduce_scatter_dp(): down = lax.ppermute(down, 'dp', minus)  20.1 us
    ppermute x1, waiting for transfers between devices, _reduce_scatter_dp(): same = lax.ppermute(lax.select(h == 0, up, down), 'dp', within)  19.3 us
    all_to_all x1, starting transfers between devices, _step(): lax.all_to_all(state, 'shard', split_axis=5, concat_axis=3, tiled=True)  9.65 us
    ppermute x2, waiting for transfers between devices, _all_gather_dp(): up = lax.ppermute(up, 'dp', plus)  8.4 us
    all_to_all x1, starting transfers between devices, _step(): lax.all_to_all(moved, 'shard', split_axis=2, concat_axis=4, tiled=True)  7.78 us
    ppermute x2, starting transfers between devices, _all_gather_dp(): down = lax.ppermute(down, 'dp', minus)  7.47 us
    ppermute x1, waiting for transfers between devices, _all_gather_dp(): other = lax.ppermute(mine, 'dp', partner)  5.99 us
    ppermute x2, waiting for transfers between devices, _reduce_scatter_dp(): up = lax.ppermute(up, 'dp', plus)  4.91 us
  transfers between devices with their start and end apart: 16, of which 9 were waited for; matrix products, arithmetic and copies ran while one was open for 10% of the time, Pallas kernels for 0%

profile of v4, /device:TPU:32, one launch (start us, length us, event | category | flops | bytes accessed | tf_op | source)
XLA Modules:
  0.0 133.2 jit_solution(1825974036834248396)
XLA Ops:
  3.3 2.1 %copy.66 = f32[3,1,2,1,16,32,128]{6,4,2,3,1,0,5:T(8,128)} copy(f32[3,1,2,1,16,32,128]{6,5,0,4,2,3,1:T(8,128)S(1)} %pad_maximum_fusion) | data formatting | bytes 3145728 | tf_op jit(solution)/shard_map/stack | solution.py:91
  5.3 9.7 %all-to-all-start.1 = ((f32[3,1,2,1,16,32,128]{6,4,2,3,1,0,5:T(8,128)}), f32[3,1,2,1,16,32,128]{6,4,2,3,1,0,5:T(8,128)S(1)}, u32[]{:S(2)}, u32[]{:S(2)}) async-start(f32[3,1,2,1,16,32,128]{6,4,2,3,1,0,5:T(8,128)} %copy.66), calls=%async_computation.1 | async-start | bytes 3145728 | tf_op jit(solution)/shard_map/all_to_all | solution.py:92
  15.1 2.3 %dynamic-slice_bitcast_fusion = (f32[2,512,128]{2,1,0:T(8,128)S(1)}, f32[2,512,128]{2,1,0:T(8,128)}, f32[2,512,128]{2,1,0:T(8,128)S(1)}) fusion(f32[2,8,512,128]{3,2,1,0:T(8,128)} %bitcast.100, s32[]{:T(128)S(6)} %select_n.139, s32[]{:T(128)S(6)} %select_n.132, s32[]{:T(128)S(6)} %select_n.126), kind=kLoop, calls=%fused_computation.15 | loop fusion | bytes 3145740 | tf_op jit(solution)/shard_map/jit(dynamic_index_in_dim)/squeeze | solution.py:16
  17.3 3.0 %collective-permute-start.2 = (f32[2,512,128]{2,1,0:T(8,128)}, f32[2,512,128]{2,1,0:T(8,128)}, u32[]{:S(2)}, u32[]{:S(2)}) collective-permute-start(f32[2,512,128]{2,1,0:T(8,128)} %get-tuple-element.21), channel_id=1, source_target_pairs={{0,192},{32,224},{64,0},{96,32},{128,64},{160,96},{192,128},{224,1... | collective-permute-start | bytes 1572872 | tf_op jit(solution)/shard_map/ppermute | solution.py:29
  20.3 11.8 %collective-permute-done.2 = f32[2,512,128]{2,1,0:T(8,128)} collective-permute-done((f32[2,512,128]{2,1,0:T(8,128)}, f32[2,512,128]{2,1,0:T(8,128)}, u32[]{:S(2)}, u32[]{:S(2)}) %collective-permute-start.2) | collective-permute-done | bytes 524320 | tf_op jit(solution)/shard_map/ppermute | solution.py:29
  32.1 3.2 %collective-permute-done = f32[2,512,128]{2,1,0:T(8,128)} collective-permute-done((f32[2,512,128]{2,1,0:T(8,128)S(1)}, f32[2,512,128]{2,1,0:T(8,128)}, u32[]{:S(2)}, u32[]{:S(2)}) %collective-permute-start) | collective-permute-done | bytes 524320 | tf_op jit(solution)/shard_map/ppermute | solution.py:28
  35.3 2.6 %bitcast_add_fusion.1 = (f32[2,512,128]{2,1,0:T(8,128)}, f32[2,512,128]{2,1,0:T(8,128)}) fusion(f32[2,512,128]{2,1,0:T(8,128)} %collective-permute-done.2, f32[2,8,512,128]{3,2,1,0:T(8,128)} %bitcast.101, s32[]{:T(128)S(6)} %select_n.134, f32[2,512,128]{2,1,0:T(8,128)} %collective-permute-done, s32[]{:T(128)S(6)} %select_n.128), kind=kLoop, calls=%fused_computation.7 | loop fusion | flops 262144 | bytes 3145736 | tf_op jit(solution)/shard_map/add | solution.py:31
  38.4 1.5 %collective-permute-start.1 = (f32[2,512,128]{2,1,0:T(8,128)}, f32[2,512,128]{2,1,0:T(8,128)}, u32[]{:S(2)}, u32[]{:S(2)}) collective-permute-start(f32[2,512,128]{2,1,0:T(8,128)} %get-tuple-element.24), channel_id=1, source_target_pairs={{0,64},{32,96},{64,128},{96,160},{128,192},{160,224},{192,0},{224,... | collective-permute-start | bytes 1572872 | tf_op jit(solution)/shard_map/ppermute | solution.py:28
  39.9 2.7 %collective-permute-start.6 = (f32[2,512,128]{2,1,0:T(8,128)S(1)}, f32[2,512,128]{2,1,0:T(8,128)S(1)}, u32[]{:S(2)}, u32[]{:S(2)}) collective-permute-start(f32[2,512,128]{2,1,0:T(8,128)S(1)} %get-tuple-element.20), channel_id=1, source_target_pairs={{0,32},{32,0},{64,96},{96,64},{128,160},{160,128},{192,224},{224,1... | collective-permute-start | bytes 1572872 | tf_op jit(solution)/shard_map/ppermute | solution.py:24
  42.7 8.4 %collective-permute-done.3 = f32[2,512,128]{2,1,0:T(8,128)} collective-permute-done((f32[2,512,128]{2,1,0:T(8,128)}, f32[2,512,128]{2,1,0:T(8,128)}, u32[]{:S(2)}, u32[]{:S(2)}) %collective-permute-start.3) | collective-permute-done | bytes 524320 | tf_op jit(solution)/shard_map/ppermute | solution.py:29
  51.0 1.7 %collective-permute-done.1 = f32[2,512,128]{2,1,0:T(8,128)} collective-permute-done((f32[2,512,128]{2,1,0:T(8,128)}, f32[2,512,128]{2,1,0:T(8,128)}, u32[]{:S(2)}, u32[]{:S(2)}) %collective-permute-start.1) | collective-permute-done | bytes 524320 | tf_op jit(solution)/shard_map/ppermute | solution.py:28
  52.7 2.6 %broadcast_select_fusion.3 = (f32[2,512,128]{2,1,0:T(8,128)}, f32[2,512,128]{2,1,0:T(8,128)}) fusion(pred[]{:T(512)S(6)} %eq.35, f32[2,512,128]{2,1,0:T(8,128)} %collective-permute-done.1, f32[2,8,512,128]{3,2,1,0:T(8,128)} %bitcast.102, s32[]{:T(128)S(6)} %select_n.130, f32[2,512,128]{2,1,0:T(8,128)} %collective-permute-done.3, s32[]{:T(128)S(6)} %select_n.136), kind=kLoop, calls=%fused_computation.30 | loop fusion | flops 524288 | bytes 3145737 | tf_op jit(solution)/shard_map/select_n | solution.py:36
  55.4 3.1 %collective-permute-start.5 = (f32[2,512,128]{2,1,0:T(8,128)}, f32[2,512,128]{2,1,0:T(8,128)}, u32[]{:S(2)}, u32[]{:S(2)}) collective-permute-start(f32[2,512,128]{2,1,0:T(8,128)} %get-tuple-element.19), channel_id=1, source_target_pairs={{32,64},{96,128},{160,192},{224,0},{0,224},{64,32},{128,96},{192,1... | collective-permute-start | bytes 1572872 | tf_op jit(solution)/shard_map/ppermute | solution.py:37
  60.8 19.3 %collective-permute-done.4 = f32[2,512,128]{2,1,0:T(8,128)} collective-permute-done((f32[2,512,128]{2,1,0:T(8,128)}, f32[2,512,128]{2,1,0:T(8,128)}, u32[]{:S(2)}, u32[]{:S(2)}) %collective-permute-start.4) | collective-permute-done | bytes 524320 | tf_op jit(solution)/shard_map/ppermute | solution.py:36
  80.5 3.4 %bitcast_dynamic-update-slice_fusion.7 = (bf16[2,4,2,512,128]{4,3,0,2,1:T(8,128)(2,1)S(1)}, bf16[2,512,128]{2,1,0:T(8,128)(2,1)}, f32[2,512,128]{2,1,0:T(8,128)S(1)}) fusion(bf16[2,4,2,512,128]{4,3,0,2,1:T(8,128)(2,1)S(1)} %broadcast_in_dim.28, s32[]{:T(128)S(6)} %select_n.140, s32[]{:T(128)S(6)} %select_n.141, f32[2,512,128]{2,1,0:T(8,128)S(1)} %bitcast.106, ...), kind=kLoop, calls=%fused_computation.25 | loop fusion | flops 2359296 | bytes 4718616 | tf_op jit(solution)/shard_map/dynamic_update_slice | solution.py:57
  85.4 3.5 %collective-permute-start.9 = (bf16[2,512,128]{2,1,0:T(8,128)(2,1)}, bf16[2,512,128]{2,1,0:T(8,128)(2,1)}, u32[]{:S(2)}, u32[]{:S(2)}) collective-permute-start(bf16[2,512,128]{2,1,0:T(8,128)(2,1)} %get-tuple-element.13), channel_id=1, source_target_pairs={{0,96},{64,160},{128,224},{192,32},{32,192},{96,0},{160,64},{224,1... | collective-permute-start | bytes 786440 | tf_op jit(solution)/shard_map/ppermute | solution.py:53
  88.8 6.0 %collective-permute-done.7 = bf16[2,512,128]{2,1,0:T(8,128)(2,1)} collective-permute-done((bf16[2,512,128]{2,1,0:T(8,128)(2,1)}, bf16[2,512,128]{2,1,0:T(8,128)(2,1)}, u32[]{:S(2)}, u32[]{:S(2)}) %collective-permute-start.7) | collective-permute-done | bytes 262176 | tf_op jit(solution)/shard_map/ppermute | solution.py:51
  97.0 1.8 %bitcast_dynamic-update-slice_fusion.4 = (bf16[2,4,2,512,128]{4,3,0,2,1:T(8,128)(2,1)S(1)}, bf16[2,512,128]{2,1,0:T(8,128)(2,1)}) fusion(bf16[2,4,2,512,128]{4,3,0,2,1:T(8,128)(2,1)S(1)} %get-tuple-element.10, s32[]{:T(128)S(6)} %select_n.146, bf16[2,512,128]{2,1,0:T(8,128)(2,1)} %collective-permute-done.9, ...), kind=kLoop, calls=%fused_computation.22 | loop fusion | flops 131072 | bytes 1048581 | tf_op jit(solution)/shard_map/dynamic_update_slice | solution.py:64
  98.8 4.2 %collective-permute-start.11 = (bf16[2,512,128]{2,1,0:T(8,128)(2,1)}, bf16[2,512,128]{2,1,0:T(8,128)(2,1)S(1)}, u32[]{:S(2)}, u32[]{:S(2)}) collective-permute-start(bf16[2,512,128]{2,1,0:T(8,128)(2,1)} %get-tuple-element.9), channel_id=1, source_target_pairs={{0,192},{32,224},{64,0},{96,32},{128,64},{160,96},{192,128},{224,1... | collective-permute-start | bytes 786440 | tf_op jit(solution)/shard_map/ppermute | solution.py:62
  103.8 7.8 %all-to-all-start = ((f32[1,2,32,16,1,128]{5,3,1,4,0,2:T(8,128)}), f32[1,2,32,16,1,128]{5,3,1,4,0,2:T(8,128)S(1)}, u32[]{:S(2)}, u32[]{:S(2)}) async-start(f32[1,2,32,16,1,128]{5,3,1,4,0,2:T(8,128)} %copy.61), calls=%async_computation | async-start | bytes 1048576 | tf_op jit(solution)/shard_map/all_to_all | solution.py:101
  111.6 3.3 %collective-permute-start.13 = (bf16[2,512,128]{2,1,0:T(8,128)(2,1)S(1)}, bf16[2,512,128]{2,1,0:T(8,128)(2,1)S(1)}, u32[]{:S(2)}, u32[]{:S(2)}) collective-permute-start(bf16[2,512,128]{2,1,0:T(8,128)(2,1)S(1)} %collective-permute-done.11), channel_id=1, source_target_pairs={{0,192},{32,224},{64,0},{96,32},{128,64},{160,96},{192,128},{224,1... | collective-permute-start | bytes 786440 | tf_op jit(solution)/shard_map/ppermute | solution.py:62
  116.0 8.4 %collective-permute-done.12 = bf16[2,512,128]{2,1,0:T(8,128)(2,1)S(1)} collective-permute-done((bf16[2,512,128]{2,1,0:T(8,128)(2,1)}, bf16[2,512,128]{2,1,0:T(8,128)(2,1)S(1)}, u32[]{:S(2)}, u32[]{:S(2)}) %collective-permute-start.12) | collective-permute-done | bytes 262176 | tf_op jit(solution)/shard_map/ppermute | solution.py:61
  126.7 2.7 %all-to-all-done = f32[1,2,32,16,1,128]{5,3,1,4,0,2:T(8,128)S(1)} async-done(((f32[1,2,32,16,1,128]{5,3,1,4,0,2:T(8,128)}), f32[1,2,32,16,1,128]{5,3,1,4,0,2:T(8,128)S(1)}, u32[]{:S(2)}, u32[]{:S(2)}) %all-to-all-start) | async-done | bytes 524320 | tf_op jit(solution)/shard_map/all_to_all | solution.py:101
  129.6 3.6 %multiply_subtract_fusion = (f32[1,2,16,4096]{3,2,1,0:T(8,128)}, f32[1,2,16,4096]{3,2,1,0:T(8,128)}, f32[1,2,16,4096]{3,2,1,0:T(8,128)}) fusion(f32[1,2,16,4096]{3,2,1,0:T(8,128)S(1)} %copy-done, f32[]{:T(128)} %bitcast.15, f32[]{:T(128)} %bitcast.14, f32[]{:T(128)} %fusion.2, f32[1,2,16,4096]{3,0,2,1:T(1,128)S(1)} %bitcast.111, ...), kind=kLoop, calls=%fused_computation.13 | loop fusion | flops 1966080 | bytes 3670028 | tf_op jit(solution)/shard_map/sub | solution.py:72
  (39 shorter events, 12.6 us)
Async XLA Ops:
  0.6 2.4 %copy-start = (f32[1,2,16,4096]{3,2,1,0:T(8,128)S(1)}, f32[1,2,16,4096]{3,2,1,0:T(8,128)}, u32[]{:S(2)}) copy-start(f32[1,2,16,4096]{3,2,1,0:T(8,128)} %param.8) | copy-start | bytes 1572868
  5.3 55.1 %all-to-all-start.1 = ((f32[3,1,2,1,16,32,128]{6,4,2,3,1,0,5:T(8,128)}), f32[3,1,2,1,16,32,128]{6,4,2,3,1,0,5:T(8,128)S(1)}, u32[]{:S(2)}, u32[]{:S(2)}) async-start(f32[3,1,2,1,16,32,128]{6,4,2,3,1,0,5:T(8,128)} %copy.66), calls=%async_computation.1 | async-start | bytes 3145728 | tf_op jit(solution)/shard_map/all_to_all | solution.py:92
  17.3 14.8 %collective-permute-start.2 = (f32[2,512,128]{2,1,0:T(8,128)}, f32[2,512,128]{2,1,0:T(8,128)}, u32[]{:S(2)}, u32[]{:S(2)}) collective-permute-start(f32[2,512,128]{2,1,0:T(8,128)} %get-tuple-element.21), channel_id=1, source_target_pairs={{0,192},{32,224},{64,0},{96,32},{128,64},{160,96},{192,128},{224,1... | collective-permute-start | bytes 1572872 | tf_op jit(solution)/shard_map/ppermute | solution.py:29
  20.3 15.0 %collective-permute-start = (f32[2,512,128]{2,1,0:T(8,128)S(1)}, f32[2,512,128]{2,1,0:T(8,128)}, u32[]{:S(2)}, u32[]{:S(2)}) collective-permute-start(f32[2,512,128]{2,1,0:T(8,128)S(1)} %get-tuple-element.22), channel_id=1, source_target_pairs={{0,64},{32,96},{64,128},{96,160},{128,192},{160,224},{192,0},{224,... | collective-permute-start | bytes 1572872 | tf_op jit(solution)/shard_map/ppermute | solution.py:28
  37.9 21.9 %copy-start.2 = (f32[64]{0:T(128)S(1)}, f32[64]{0:T(128)}, u32[]{:S(2)}) copy-start(f32[64]{0:T(128)} %param.12) | copy-start | bytes 772
  37.9 13.1 %collective-permute-start.3 = (f32[2,512,128]{2,1,0:T(8,128)}, f32[2,512,128]{2,1,0:T(8,128)}, u32[]{:S(2)}, u32[]{:S(2)}) collective-permute-start(f32[2,512,128]{2,1,0:T(8,128)} %get-tuple-element.23), channel_id=1, source_target_pairs={{0,192},{32,224},{64,0},{96,32},{128,64},{160,96},{192,128},{224,1... | collective-permute-start | bytes 1572872 | tf_op jit(solution)/shard_map/ppermute | solution.py:29
  38.4 14.3 %collective-permute-start.1 = (f32[2,512,128]{2,1,0:T(8,128)}, f32[2,512,128]{2,1,0:T(8,128)}, u32[]{:S(2)}, u32[]{:S(2)}) collective-permute-start(f32[2,512,128]{2,1,0:T(8,128)} %get-tuple-element.24), channel_id=1, source_target_pairs={{0,64},{32,96},{64,128},{96,160},{128,192},{160,224},{192,0},{224,... | collective-permute-start | bytes 1572872 | tf_op jit(solution)/shard_map/ppermute | solution.py:28
  39.9 20.8 %collective-permute-start.6 = (f32[2,512,128]{2,1,0:T(8,128)S(1)}, f32[2,512,128]{2,1,0:T(8,128)S(1)}, u32[]{:S(2)}, u32[]{:S(2)}) collective-permute-start(f32[2,512,128]{2,1,0:T(8,128)S(1)} %get-tuple-element.20), channel_id=1, source_target_pairs={{0,32},{32,0},{64,96},{96,64},{128,160},{160,128},{192,224},{224,1... | collective-permute-start | bytes 1572872 | tf_op jit(solution)/shard_map/ppermute | solution.py:24
  55.3 24.7 %collective-permute-start.4 = (f32[2,512,128]{2,1,0:T(8,128)}, f32[2,512,128]{2,1,0:T(8,128)}, u32[]{:S(2)}, u32[]{:S(2)}) collective-permute-start(f32[2,512,128]{2,1,0:T(8,128)} %get-tuple-element.18), channel_id=1, source_target_pairs={{0,64},{64,128},{128,192},{192,0},{32,224},{96,32},{160,96},{224,1... | collective-permute-start | bytes 1572872 | tf_op jit(solution)/shard_map/ppermute | solution.py:36
  55.4 24.7 %collective-permute-start.5 = (f32[2,512,128]{2,1,0:T(8,128)}, f32[2,512,128]{2,1,0:T(8,128)}, u32[]{:S(2)}, u32[]{:S(2)}) collective-permute-start(f32[2,512,128]{2,1,0:T(8,128)} %get-tuple-element.19), channel_id=1, source_target_pairs={{32,64},{96,128},{160,192},{224,0},{0,224},{64,32},{128,96},{192,1... | collective-permute-start | bytes 1572872 | tf_op jit(solution)/shard_map/ppermute | solution.py:37
  60.8 19.3 %copy-start.1 = (f32[2,512,128]{2,1,0:T(8,128)}, f32[2,512,128]{2,1,0:T(8,128)S(1)}, u32[]{:S(2)}) copy-start(f32[2,512,128]{2,1,0:T(8,128)S(1)} %collective-permute-done.6) | copy-start | bytes 1572868
  83.8 11.0 %collective-permute-start.7 = (bf16[2,512,128]{2,1,0:T(8,128)(2,1)}, bf16[2,512,128]{2,1,0:T(8,128)(2,1)}, u32[]{:S(2)}, u32[]{:S(2)}) collective-permute-start(bf16[2,512,128]{2,1,0:T(8,128)(2,1)} %get-tuple-element.13), channel_id=1, source_target_pairs={{0,32},{32,0},{64,96},{96,64},{128,160},{160,128},{192,224},{224,1... | collective-permute-start | bytes 786440 | tf_op jit(solution)/shard_map/ppermute | solution.py:51
  85.4 10.5 %collective-permute-start.8 = (bf16[2,512,128]{2,1,0:T(8,128)(2,1)}, bf16[2,512,128]{2,1,0:T(8,128)(2,1)S(1)}, u32[]{:S(2)}, u32[]{:S(2)}) collective-permute-start(bf16[2,512,128]{2,1,0:T(8,128)(2,1)} %get-tuple-element.13), channel_id=1, source_target_pairs={{0,64},{64,128},{128,192},{192,0},{32,224},{96,32},{160,96},{224,1... | collective-permute-start | bytes 786440 | tf_op jit(solution)/shard_map/ppermute | solution.py:52
  85.4 10.8 %collective-permute-start.9 = (bf16[2,512,128]{2,1,0:T(8,128)(2,1)}, bf16[2,512,128]{2,1,0:T(8,128)(2,1)}, u32[]{:S(2)}, u32[]{:S(2)}) collective-permute-start(bf16[2,512,128]{2,1,0:T(8,128)(2,1)} %get-tuple-element.13), channel_id=1, source_target_pairs={{0,96},{64,160},{128,224},{192,32},{32,192},{96,0},{160,64},{224,1... | collective-permute-start | bytes 786440 | tf_op jit(solution)/shard_map/ppermute | solution.py:53
  98.8 12.9 %collective-permute-start.11 = (bf16[2,512,128]{2,1,0:T(8,128)(2,1)}, bf16[2,512,128]{2,1,0:T(8,128)(2,1)S(1)}, u32[]{:S(2)}, u32[]{:S(2)}) collective-permute-start(bf16[2,512,128]{2,1,0:T(8,128)(2,1)} %get-tuple-element.9), channel_id=1, source_target_pairs={{0,192},{32,224},{64,0},{96,32},{128,64},{160,96},{192,128},{224,1... | collective-permute-start | bytes 786440 | tf_op jit(solution)/shard_map/ppermute | solution.py:62
  102.9 12.0 %collective-permute-start.10 = (bf16[2,512,128]{2,1,0:T(8,128)(2,1)}, bf16[2,512,128]{2,1,0:T(8,128)(2,1)}, u32[]{:S(2)}, u32[]{:S(2)}) collective-permute-start(bf16[2,512,128]{2,1,0:T(8,128)(2,1)} %get-tuple-element.11), channel_id=1, source_target_pairs={{0,64},{32,96},{64,128},{96,160},{128,192},{160,224},{192,0},{224,... | collective-permute-start | bytes 786440 | tf_op jit(solution)/shard_map/ppermute | solution.py:61
  103.8 25.5 %all-to-all-start = ((f32[1,2,32,16,1,128]{5,3,1,4,0,2:T(8,128)}), f32[1,2,32,16,1,128]{5,3,1,4,0,2:T(8,128)S(1)}, u32[]{:S(2)}, u32[]{:S(2)}) async-start(f32[1,2,32,16,1,128]{5,3,1,4,0,2:T(8,128)} %copy.61), calls=%async_computation | async-start | bytes 1048576 | tf_op jit(solution)/shard_map/all_to_all | solution.py:101
  111.6 14.3 %collective-permute-start.13 = (bf16[2,512,128]{2,1,0:T(8,128)(2,1)S(1)}, bf16[2,512,128]{2,1,0:T(8,128)(2,1)S(1)}, u32[]{:S(2)}, u32[]{:S(2)}) collective-permute-start(bf16[2,512,128]{2,1,0:T(8,128)(2,1)S(1)} %collective-permute-done.11), channel_id=1, source_target_pairs={{0,192},{32,224},{64,0},{96,32},{128,64},{160,96},{192,128},{224,1... | collective-permute-start | bytes 786440 | tf_op jit(solution)/shard_map/ppermute | solution.py:62
  115.0 9.5 %collective-permute-start.12 = (bf16[2,512,128]{2,1,0:T(8,128)(2,1)}, bf16[2,512,128]{2,1,0:T(8,128)(2,1)S(1)}, u32[]{:S(2)}, u32[]{:S(2)}) collective-permute-start(bf16[2,512,128]{2,1,0:T(8,128)(2,1)} %collective-permute-done.10), channel_id=1, source_target_pairs={{0,64},{32,96},{64,128},{96,160},{128,192},{160,224},{192,0},{224,... | collective-permute-start | bytes 786440 | tf_op jit(solution)/shard_map/ppermute | solution.py:61

commit v5 on v1

--- a/solution.py
+++ b/solution.py
@@ -21,16 +21,21 @@
     d = lax.axis_index("dp")
     y = d // 2
     h = d % 2
+    raw = lax.ppermute(_take(x, 2 * y + 1 - h), "dp", partner)
     up = _take(x, 2 * ((y - 1) % ring))
     down = _take(x, 2 * ((y + 1) % ring) + 1)
-    for t in range(ring - 1):
+    for t in range(ring - 2):
         up = lax.ppermute(up, "dp", plus)
         down = lax.ppermute(down, "dp", minus)
         up = up + _take(x, 2 * ((y - t - 2) % ring))
         down = down + _take(x, 2 * ((y + t + 2) % ring) + 1)
-    keep = lax.select(h == 0, up, down)
-    send = lax.select(h == 0, down, up)
-    return keep + lax.ppermute(send, "dp", partner)
+    within = [(2 * r, 2 * ((r + 1) % ring)) for r in range(ring)]
+    within += [(2 * r + 1, 2 * ((r - 1) % ring) + 1) for r in range(ring)]
+    across = [(2 * r + 1, 2 * ((r + 1) % ring)) for r in range(ring)]
+    across += [(2 * r, 2 * ((r - 1) % ring) + 1) for r in range(ring)]
+    same = lax.ppermute(lax.select(h == 0, up, down), "dp", within)
+    other = lax.ppermute(lax.select(h == 0, down, up), "dp", across)
+    return (_take(x, 2 * y + h) + same) + (other + raw)
 
 
 def _all_gather_dp(mine, groups):

time: 128 us -> 126 us (0.984)
  waiting for transfers between devices: 53 us -> 50.6 us
    ppermute x3 -> x2, waiting for transfers between devices: 33.3 us -> 20.7 us  [_reduce_scatter_dp(): up = lax.ppermute(up, 'dp', plus)]
    ppermute x1 -> x3, waiting for transfers between devices: 7.91 us -> 17.1 us  [the longest x1 17.1 us: _reduce_scatter_dp(): same = lax.ppermute(lax.select(h == 0, up, down), 'dp', within)]
    ppermute x1 -> x3, starting transfers between devices: 2.73 us -> 8.27 us  [the longest x1 4.5 us: _reduce_scatter_dp(): other = lax.ppermute(lax.select(h == 0, down, up), 'dp', across)]
    ppermute x3 -> x2, starting transfers between devices: 5.3 us -> 3.32 us  [_reduce_scatter_dp(): down = lax.ppermute(down, 'dp', minus)]
    ppermute x3 -> x2, starting transfers between devices: 4.56 us -> 3.23 us  [_reduce_scatter_dp(): up = lax.ppermute(up, 'dp', plus)]
    add x2 -> x1, other arithmetic: 3.72 us -> 2.59 us  [_reduce_scatter_dp(): down = down + _take(x, 2 * ((y + t + 2) % ring) + 1)]
  transfers between devices with their start and end apart: 16 -> 16, of which waited for: 8 -> 6; matrix products, arithmetic and copies ran while one was open for 15% -> 14% of each run, Pallas kernels for 0% -> 0%
where the time goes in v5:
time: 126 us; the launch traced here: 125 us
  waiting for transfers between devices  50.6 us (40%)
  starting transfers between devices  44.3 us (35%)
  local copies, waits for them, and re-layouts  14.1 us (11%)
  other arithmetic  13.7 us (11%)
  between operations  2.29 us (2%)
    ppermute x2, waiting for transfers between devices, _reduce_scatter_dp(): up = lax.ppermute(up, 'dp', plus)  20.7 us
    ppermute x1, waiting for transfers between devices, _reduce_scatter_dp(): same = lax.ppermute(lax.select(h == 0, up, down), 'dp', within)  17.1 us
    ppermute x3, starting transfers between devices, _all_gather_dp(): down = lax.ppermute(down, 'dp', minus)  9.68 us
    all_to_all x1, starting transfers between devices, _step(): lax.all_to_all(state, 'shard', split_axis=5, concat_axis=3, tiled=True)  9.65 us
    all_to_all x1, starting transfers between devices, _step(): lax.all_to_all(moved, 'shard', split_axis=2, concat_axis=4, tiled=True)  8.23 us
    ppermute x1, waiting for transfers between devices, _all_gather_dp(): other = lax.ppermute(mine, 'dp', partner)  6.17 us
    ppermute x3, waiting for transfers between devices, _all_gather_dp(): up = lax.ppermute(up, 'dp', plus)  4.64 us
    ppermute x1, starting transfers between devices, _reduce_scatter_dp(): other = lax.ppermute(lax.select(h == 0, down, up), 'dp', across)  4.5 us
  transfers between devices with their start and end apart: 16, of which 6 were waited for; matrix products, arithmetic and copies ran while one was open for 14% of the time, Pallas kernels for 0%

profile of v5, /device:TPU:32, one launch (start us, length us, event | category | flops | bytes accessed | tf_op | source)
XLA Modules:
  0.0 125.0 jit_solution(17084194728434908614)
XLA Ops:
  3.3 2.1 %copy.64 = f32[3,1,2,1,16,32,128]{6,4,2,3,1,0,5:T(8,128)} copy(f32[3,1,2,1,16,32,128]{6,5,0,4,2,3,1:T(8,128)S(1)} %pad_maximum_fusion) | data formatting | bytes 3145728 | tf_op jit(solution)/shard_map/stack | solution.py:84
  5.3 9.7 %all-to-all-start.1 = ((f32[3,1,2,1,16,32,128]{6,4,2,3,1,0,5:T(8,128)}), f32[3,1,2,1,16,32,128]{6,4,2,3,1,0,5:T(8,128)S(1)}, u32[]{:S(2)}, u32[]{:S(2)}) async-start(f32[3,1,2,1,16,32,128]{6,4,2,3,1,0,5:T(8,128)} %copy.64), calls=%async_computation.1 | async-start | bytes 3145728 | tf_op jit(solution)/shard_map/all_to_all | solution.py:85
  15.1 1.5 %dynamic-slice_bitcast_fusion = (f32[2,512,128]{2,1,0:T(8,128)S(1)}, f32[2,512,128]{2,1,0:T(8,128)S(1)}, f32[2,512,128]{2,1,0:T(8,128)S(1)}) fusion(f32[2,8,512,128]{3,2,1,0:T(8,128)} %bitcast.102, s32[]{:T(128)S(6)} %select_n.132, s32[]{:T(128)S(6)} %select_n.125, s32[]{:T(128)S(6)} %select_n.119), kind=kLoop, calls=%fused_computation.17 | loop fusion | bytes 3145740 | tf_op jit(solution)/shard_map/jit(dynamic_index_in_dim)/squeeze | solution.py:16
  16.5 1.7 %collective-permute-start = (f32[2,512,128]{2,1,0:T(8,128)S(1)}, f32[2,512,128]{2,1,0:T(8,128)}, u32[]{:S(2)}, u32[]{:S(2)}) collective-permute-start(f32[2,512,128]{2,1,0:T(8,128)S(1)} %get-tuple-element.17), channel_id=1, source_target_pairs={{0,64},{32,96},{64,128},{96,160},{128,192},{160,224},{192,0},{224,... | collective-permute-start | bytes 1572872 | tf_op jit(solution)/shard_map/ppermute | solution.py:28
  18.2 1.7 %collective-permute-start.2 = (f32[2,512,128]{2,1,0:T(8,128)S(1)}, f32[2,512,128]{2,1,0:T(8,128)}, u32[]{:S(2)}, u32[]{:S(2)}) collective-permute-start(f32[2,512,128]{2,1,0:T(8,128)S(1)} %get-tuple-element.16), channel_id=1, source_target_pairs={{0,192},{32,224},{64,0},{96,32},{128,64},{160,96},{192,128},{224,1... | collective-permute-start | bytes 1572872 | tf_op jit(solution)/shard_map/ppermute | solution.py:29
  19.8 12.1 %collective-permute-done = f32[2,512,128]{2,1,0:T(8,128)} collective-permute-done((f32[2,512,128]{2,1,0:T(8,128)S(1)}, f32[2,512,128]{2,1,0:T(8,128)}, u32[]{:S(2)}, u32[]{:S(2)}) %collective-permute-start) | collective-permute-done | bytes 524320 | tf_op jit(solution)/shard_map/ppermute | solution.py:28
  32.0 2.6 %bitcast_add_fusion.1 = (f32[2,512,128]{2,1,0:T(8,128)}, f32[2,512,128]{2,1,0:T(8,128)}) fusion(f32[2,512,128]{2,1,0:T(8,128)} %collective-permute-done.2, f32[2,8,512,128]{3,2,1,0:T(8,128)} %bitcast.103, s32[]{:T(128)S(6)} %select_n.127, f32[2,512,128]{2,1,0:T(8,128)} %collective-permute-done, s32[]{:T(128)S(6)} %select_n.121), kind=kLoop, calls=%fused_computation.9 | loop fusion | flops 262144 | bytes 3145736 | tf_op jit(solution)/shard_map/add | solution.py:31
  34.5 1.6 %collective-permute-start.1 = (f32[2,512,128]{2,1,0:T(8,128)}, f32[2,512,128]{2,1,0:T(8,128)S(1)}, u32[]{:S(2)}, u32[]{:S(2)}) collective-permute-start(f32[2,512,128]{2,1,0:T(8,128)} %get-tuple-element.19), channel_id=1, source_target_pairs={{0,64},{32,96},{64,128},{96,160},{128,192},{160,224},{192,0},{224,... | collective-permute-start | bytes 1572872 | tf_op jit(solution)/shard_map/ppermute | solution.py:28
  36.1 1.7 %collective-permute-start.3 = (f32[2,512,128]{2,1,0:T(8,128)}, f32[2,512,128]{2,1,0:T(8,128)S(1)}, u32[]{:S(2)}, u32[]{:S(2)}) collective-permute-start(f32[2,512,128]{2,1,0:T(8,128)} %get-tuple-element.18), channel_id=1, source_target_pairs={{0,192},{32,224},{64,0},{96,32},{128,64},{160,96},{192,128},{224,1... | collective-permute-start | bytes 1572872 | tf_op jit(solution)/shard_map/ppermute | solution.py:29
  37.8 2.7 %collective-permute-start.6 = (f32[2,512,128]{2,1,0:T(8,128)S(1)}, f32[2,512,128]{2,1,0:T(8,128)}, u32[]{:S(2)}, u32[]{:S(2)}) collective-permute-start(f32[2,512,128]{2,1,0:T(8,128)S(1)} %get-tuple-element.15), channel_id=1, source_target_pairs={{0,32},{32,0},{64,96},{96,64},{128,160},{160,128},{192,224},{224,1... | collective-permute-start | bytes 1572872 | tf_op jit(solution)/shard_map/ppermute | solution.py:24
  40.5 8.6 %collective-permute-done.1 = f32[2,512,128]{2,1,0:T(8,128)S(1)} collective-permute-done((f32[2,512,128]{2,1,0:T(8,128)}, f32[2,512,128]{2,1,0:T(8,128)S(1)}, u32[]{:S(2)}, u32[]{:S(2)}) %collective-permute-start.1) | collective-permute-done | bytes 524320 | tf_op jit(solution)/shard_map/ppermute | solution.py:28
  49.1 2.3 %broadcast_select_fusion.3 = (f32[2,512,128]{2,1,0:T(8,128)}, f32[2,512,128]{2,1,0:T(8,128)}) fusion(pred[]{:T(512)S(6)} %eq.35, f32[2,512,128]{2,1,0:T(8,128)S(1)} %collective-permute-done.1, f32[2,8,512,128]{3,2,1,0:T(8,128)} %bitcast.104, s32[]{:T(128)S(6)} %select_n.123, f32[2,512,128]{2,1,0:T(8,128)S(1)} %collective-permute-done.3, s32[]{:T(128)S(6)} %select_n.129), kind=kLoop, calls=%fused_computation.30 | loop fusion | flops 524288 | bytes 3145737 | tf_op jit(solution)/shard_map/select_n | solution.py:36
  52.4 4.5 %collective-permute-start.5 = (f32[2,512,128]{2,1,0:T(8,128)}, f32[2,512,128]{2,1,0:T(8,128)S(1)}, u32[]{:S(2)}, u32[]{:S(2)}) collective-permute-start(f32[2,512,128]{2,1,0:T(8,128)} %get-tuple-element.14), channel_id=1, source_target_pairs={{32,64},{96,128},{160,192},{224,0},{0,224},{64,32},{128,96},{192,1... | collective-permute-start | bytes 1572872 | tf_op jit(solution)/shard_map/ppermute | solution.py:37
  59.3 17.1 %collective-permute-done.4 = f32[2,512,128]{2,1,0:T(8,128)S(1)} collective-permute-done((f32[2,512,128]{2,1,0:T(8,128)}, f32[2,512,128]{2,1,0:T(8,128)S(1)}, u32[]{:S(2)}, u32[]{:S(2)}) %collective-permute-start.4) | collective-permute-done | bytes 524320 | tf_op jit(solution)/shard_map/ppermute | solution.py:36
  76.4 2.4 %subtract_convert_fusion = (bf16[2,512,128]{2,1,0:T(8,128)(2,1)S(1)}, f32[2,512,128]{2,1,0:T(8,128)S(1)}) fusion(f32[2,512,128]{2,1,0:T(8,128)S(1)} %bitcast.117, f32[2,512,128]{2,1,0:T(8,128)S(1)} %bitcast.116, f32[2,512,128]{2,1,0:T(8,128)S(1)} %bitcast.115, f32[]{:T(128)} %bitcast.15, f32[]{:T(128)} %bitcast.14, f32[]{:T(128)} %fusion.3, ...), kind=kLoop, calls=%fused_computation.14 | loop fusion | flops 2359296 | bytes 4456464 | tf_op jit(solution)/shard_map/convert_element_type | solution.py:91
  78.8 1.8 %collective-permute-start.7 = (bf16[2,512,128]{2,1,0:T(8,128)(2,1)S(1)}, bf16[2,512,128]{2,1,0:T(8,128)(2,1)S(1)}, u32[]{:S(2)}, u32[]{:S(2)}) collective-permute-start(bf16[2,512,128]{2,1,0:T(8,128)(2,1)S(1)} %get-tuple-element.8), channel_id=1, source_target_pairs={{0,32},{32,0},{64,96},{96,64},{128,160},{160,128},{192,224},{224,1... | collective-permute-start | bytes 786440 | tf_op jit(solution)/shard_map/ppermute | solution.py:46
  80.6 6.2 %collective-permute-done.7 = bf16[2,512,128]{2,1,0:T(8,128)(2,1)S(1)} collective-permute-done((bf16[2,512,128]{2,1,0:T(8,128)(2,1)S(1)}, bf16[2,512,128]{2,1,0:T(8,128)(2,1)S(1)}, u32[]{:S(2)}, u32[]{:S(2)}) %collective-permute-start.7) | collective-permute-done | bytes 262176 | tf_op jit(solution)/shard_map/ppermute | solution.py:46
  87.5 3.2 %collective-permute-start.9 = (bf16[2,512,128]{2,1,0:T(8,128)(2,1)S(1)}, bf16[2,512,128]{2,1,0:T(8,128)(2,1)}, u32[]{:S(2)}, u32[]{:S(2)}) collective-permute-start(bf16[2,512,128]{2,1,0:T(8,128)(2,1)S(1)} %get-tuple-element.24), channel_id=1, source_target_pairs={{0,192},{32,224},{64,0},{96,32},{128,64},{160,96},{192,128},{224,1... | collective-permute-start | bytes 786440 | tf_op jit(solution)/shard_map/ppermute | solution.py:55
  91.7 8.2 %all-to-all-start = ((f32[1,2,32,16,1,128]{5,3,1,4,0,2:T(8,128)}), f32[1,2,32,16,1,128]{5,3,1,4,0,2:T(8,128)S(1)}, u32[]{:S(2)}, u32[]{:S(2)}) async-start(f32[1,2,32,16,1,128]{5,3,1,4,0,2:T(8,128)} %copy.59), calls=%async_computation | async-start | bytes 1048576 | tf_op jit(solution)/shard_map/all_to_all | solution.py:94
  101.5 3.2 %collective-permute-start.11 = (bf16[2,512,128]{2,1,0:T(8,128)(2,1)}, bf16[2,512,128]{2,1,0:T(8,128)(2,1)S(1)}, u32[]{:S(2)}, u32[]{:S(2)}) collective-permute-start(bf16[2,512,128]{2,1,0:T(8,128)(2,1)} %collective-permute-done.9), channel_id=1, source_target_pairs={{0,192},{32,224},{64,0},{96,32},{128,64},{160,96},{192,128},{224,1... | collective-permute-start | bytes 786440 | tf_op jit(solution)/shard_map/ppermute | solution.py:55
  106.7 4.6 %collective-permute-done.10 = bf16[2,512,128]{2,1,0:T(8,128)(2,1)} collective-permute-done((bf16[2,512,128]{2,1,0:T(8,128)(2,1)}, bf16[2,512,128]{2,1,0:T(8,128)(2,1)}, u32[]{:S(2)}, u32[]{:S(2)}) %collective-permute-start.10) | collective-permute-done | bytes 262176 | tf_op jit(solution)/shard_map/ppermute | solution.py:54
  111.3 3.2 %collective-permute-start.13 = (bf16[2,512,128]{2,1,0:T(8,128)(2,1)S(1)}, bf16[2,512,128]{2,1,0:T(8,128)(2,1)}, u32[]{:S(2)}, u32[]{:S(2)}) collective-permute-start(bf16[2,512,128]{2,1,0:T(8,128)(2,1)S(1)} %collective-permute-done.11), channel_id=1, source_target_pairs={{0,192},{32,224},{64,0},{96,32},{128,64},{160,96},{192,128},{224,1... | collective-permute-start | bytes 786440 | tf_op jit(solution)/shard_map/ppermute | solution.py:55
  115.6 2.0 %all-to-all-done = f32[1,2,32,16,1,128]{5,3,1,4,0,2:T(8,128)S(1)} async-done(((f32[1,2,32,16,1,128]{5,3,1,4,0,2:T(8,128)}), f32[1,2,32,16,1,128]{5,3,1,4,0,2:T(8,128)S(1)}, u32[]{:S(2)}, u32[]{:S(2)}) %all-to-all-start) | async-done | bytes 524320 | tf_op jit(solution)/shard_map/all_to_all | solution.py:94
  117.9 3.6 %multiply_subtract_fusion = (f32[1,2,16,4096]{3,2,1,0:T(8,128)}, f32[1,2,16,4096]{3,2,1,0:T(8,128)}, f32[1,2,16,4096]{3,2,1,0:T(8,128)}) fusion(f32[1,2,16,4096]{3,2,1,0:T(8,128)S(1)} %copy-done.1, f32[]{:T(128)} %bitcast.15, f32[]{:T(128)} %bitcast.14, f32[]{:T(128)} %fusion.3, f32[1,2,16,4096]{3,0,2,1:T(1,128)S(1)} %bitcast.111, ...), kind=kLoop, calls=%fused_computation.15 | loop fusion | flops 1966080 | bytes 3670028 | tf_op jit(solution)/shard_map/sub | solution.py:65
  (42 shorter events, 14.6 us)
Async XLA Ops:
  0.6 2.4 %copy-start.2 = (f32[1,2,16,4096]{3,2,1,0:T(8,128)S(1)}, f32[1,2,16,4096]{3,2,1,0:T(8,128)}, u32[]{:S(2)}) copy-start(f32[1,2,16,4096]{3,2,1,0:T(8,128)} %param.10) | copy-start | bytes 1572868
  5.3 53.7 %all-to-all-start.1 = ((f32[3,1,2,1,16,32,128]{6,4,2,3,1,0,5:T(8,128)}), f32[3,1,2,1,16,32,128]{6,4,2,3,1,0,5:T(8,128)S(1)}, u32[]{:S(2)}, u32[]{:S(2)}) async-start(f32[3,1,2,1,16,32,128]{6,4,2,3,1,0,5:T(8,128)} %copy.64), calls=%async_computation.1 | async-start | bytes 3145728 | tf_op jit(solution)/shard_map/all_to_all | solution.py:85
  16.5 15.4 %collective-permute-start = (f32[2,512,128]{2,1,0:T(8,128)S(1)}, f32[2,512,128]{2,1,0:T(8,128)}, u32[]{:S(2)}, u32[]{:S(2)}) collective-permute-start(f32[2,512,128]{2,1,0:T(8,128)S(1)} %get-tuple-element.17), channel_id=1, source_target_pairs={{0,64},{32,96},{64,128},{96,160},{128,192},{160,224},{192,0},{224,... | collective-permute-start | bytes 1572872 | tf_op jit(solution)/shard_map/ppermute | solution.py:28
  18.2 13.8 %collective-permute-start.2 = (f32[2,512,128]{2,1,0:T(8,128)S(1)}, f32[2,512,128]{2,1,0:T(8,128)}, u32[]{:S(2)}, u32[]{:S(2)}) collective-permute-start(f32[2,512,128]{2,1,0:T(8,128)S(1)} %get-tuple-element.16), channel_id=1, source_target_pairs={{0,192},{32,224},{64,0},{96,32},{128,64},{160,96},{192,128},{224,1... | collective-permute-start | bytes 1572872 | tf_op jit(solution)/shard_map/ppermute | solution.py:29
  34.5 23.8 %copy-start.3 = (f32[64]{0:T(128)S(1)}, f32[64]{0:T(128)}, u32[]{:S(2)}) copy-start(f32[64]{0:T(128)} %param.12) | copy-start | bytes 772
  34.5 14.6 %collective-permute-start.1 = (f32[2,512,128]{2,1,0:T(8,128)}, f32[2,512,128]{2,1,0:T(8,128)S(1)}, u32[]{:S(2)}, u32[]{:S(2)}) collective-permute-start(f32[2,512,128]{2,1,0:T(8,128)} %get-tuple-element.19), channel_id=1, source_target_pairs={{0,64},{32,96},{64,128},{96,160},{128,192},{160,224},{192,0},{224,... | collective-permute-start | bytes 1572872 | tf_op jit(solution)/shard_map/ppermute | solution.py:28
  36.1 13.0 %collective-permute-start.3 = (f32[2,512,128]{2,1,0:T(8,128)}, f32[2,512,128]{2,1,0:T(8,128)S(1)}, u32[]{:S(2)}, u32[]{:S(2)}) collective-permute-start(f32[2,512,128]{2,1,0:T(8,128)} %get-tuple-element.18), channel_id=1, source_target_pairs={{0,192},{32,224},{64,0},{96,32},{128,64},{160,96},{192,128},{224,1... | collective-permute-start | bytes 1572872 | tf_op jit(solution)/shard_map/ppermute | solution.py:29
  37.8 21.5 %collective-permute-start.6 = (f32[2,512,128]{2,1,0:T(8,128)S(1)}, f32[2,512,128]{2,1,0:T(8,128)}, u32[]{:S(2)}, u32[]{:S(2)}) collective-permute-start(f32[2,512,128]{2,1,0:T(8,128)S(1)} %get-tuple-element.15), channel_id=1, source_target_pairs={{0,32},{32,0},{64,96},{96,64},{128,160},{160,128},{192,224},{224,1... | collective-permute-start | bytes 1572872 | tf_op jit(solution)/shard_map/ppermute | solution.py:24
  51.4 25.0 %collective-permute-start.4 = (f32[2,512,128]{2,1,0:T(8,128)}, f32[2,512,128]{2,1,0:T(8,128)S(1)}, u32[]{:S(2)}, u32[]{:S(2)}) collective-permute-start(f32[2,512,128]{2,1,0:T(8,128)} %get-tuple-element.13), channel_id=1, source_target_pairs={{0,64},{64,128},{128,192},{192,0},{32,224},{96,32},{160,96},{224,1... | collective-permute-start | bytes 1572872 | tf_op jit(solution)/shard_map/ppermute | solution.py:36
  52.4 24.0 %collective-permute-start.5 = (f32[2,512,128]{2,1,0:T(8,128)}, f32[2,512,128]{2,1,0:T(8,128)S(1)}, u32[]{:S(2)}, u32[]{:S(2)}) collective-permute-start(f32[2,512,128]{2,1,0:T(8,128)} %get-tuple-element.14), channel_id=1, source_target_pairs={{32,64},{96,128},{160,192},{224,0},{0,224},{64,32},{128,96},{192,1... | collective-permute-start | bytes 1572872 | tf_op jit(solution)/shard_map/ppermute | solution.py:37
  78.8 8.0 %collective-permute-start.7 = (bf16[2,512,128]{2,1,0:T(8,128)(2,1)S(1)}, bf16[2,512,128]{2,1,0:T(8,128)(2,1)S(1)}, u32[]{:S(2)}, u32[]{:S(2)}) collective-permute-start(bf16[2,512,128]{2,1,0:T(8,128)(2,1)S(1)} %get-tuple-element.8), channel_id=1, source_target_pairs={{0,32},{32,0},{64,96},{96,64},{128,160},{160,128},{192,224},{224,1... | collective-permute-start | bytes 786440 | tf_op jit(solution)/shard_map/ppermute | solution.py:46
  87.5 13.9 %collective-permute-start.8 = (bf16[2,512,128]{2,1,0:T(8,128)(2,1)}, bf16[2,512,128]{2,1,0:T(8,128)(2,1)}, u32[]{:S(2)}, u32[]{:S(2)}) collective-permute-start(bf16[2,512,128]{2,1,0:T(8,128)(2,1)} %get-tuple-element.23), channel_id=1, source_target_pairs={{0,64},{32,96},{64,128},{96,160},{128,192},{160,224},{192,0},{224,... | collective-permute-start | bytes 786440 | tf_op jit(solution)/shard_map/ppermute | solution.py:54
  87.5 14.0 %collective-permute-start.9 = (bf16[2,512,128]{2,1,0:T(8,128)(2,1)S(1)}, bf16[2,512,128]{2,1,0:T(8,128)(2,1)}, u32[]{:S(2)}, u32[]{:S(2)}) collective-permute-start(bf16[2,512,128]{2,1,0:T(8,128)(2,1)S(1)} %get-tuple-element.24), channel_id=1, source_target_pairs={{0,192},{32,224},{64,0},{96,32},{128,64},{160,96},{192,128},{224,1... | collective-permute-start | bytes 786440 | tf_op jit(solution)/shard_map/ppermute | solution.py:55
  91.7 26.0 %all-to-all-start = ((f32[1,2,32,16,1,128]{5,3,1,4,0,2:T(8,128)}), f32[1,2,32,16,1,128]{5,3,1,4,0,2:T(8,128)S(1)}, u32[]{:S(2)}, u32[]{:S(2)}) async-start(f32[1,2,32,16,1,128]{5,3,1,4,0,2:T(8,128)} %copy.59), calls=%async_computation | async-start | bytes 1048576 | tf_op jit(solution)/shard_map/all_to_all | solution.py:94
  100.3 17.6 %copy-start.1 = (f32[1,2,16,4096]{3,2,1,0:T(8,128)S(1)}, f32[1,2,16,4096]{3,2,1,0:T(8,128)}, u32[]{:S(2)}) copy-start(f32[1,2,16,4096]{3,2,1,0:T(8,128)} %param.8) | copy-start | bytes 1572868
  101.4 9.9 %collective-permute-start.10 = (bf16[2,512,128]{2,1,0:T(8,128)(2,1)}, bf16[2,512,128]{2,1,0:T(8,128)(2,1)}, u32[]{:S(2)}, u32[]{:S(2)}) collective-permute-start(bf16[2,512,128]{2,1,0:T(8,128)(2,1)} %collective-permute-done.8), channel_id=1, source_target_pairs={{0,64},{32,96},{64,128},{96,160},{128,192},{160,224},{192,0},{224,... | collective-permute-start | bytes 786440 | tf_op jit(solution)/shard_map/ppermute | solution.py:54
  101.5 9.8 %collective-permute-start.11 = (bf16[2,512,128]{2,1,0:T(8,128)(2,1)}, bf16[2,512,128]{2,1,0:T(8,128)(2,1)S(1)}, u32[]{:S(2)}, u32[]{:S(2)}) collective-permute-start(bf16[2,512,128]{2,1,0:T(8,128)(2,1)} %collective-permute-done.9), channel_id=1, source_target_pairs={{0,192},{32,224},{64,0},{96,32},{128,64},{160,96},{192,128},{224,1... | collective-permute-start | bytes 786440 | tf_op jit(solution)/shard_map/ppermute | solution.py:55
  111.3 10.2 %collective-permute-start.12 = (bf16[2,512,128]{2,1,0:T(8,128)(2,1)}, bf16[2,512,128]{2,1,0:T(8,128)(2,1)}, u32[]{:S(2)}, u32[]{:S(2)}) collective-permute-start(bf16[2,512,128]{2,1,0:T(8,128)(2,1)} %collective-permute-done.10), channel_id=1, source_target_pairs={{0,64},{32,96},{64,128},{96,160},{128,192},{160,224},{192,0},{224,... | collective-permute-start | bytes 786440 | tf_op jit(solution)/shard_map/ppermute | solution.py:54
  111.3 11.3 %collective-permute-start.13 = (bf16[2,512,128]{2,1,0:T(8,128)(2,1)S(1)}, bf16[2,512,128]{2,1,0:T(8,128)(2,1)}, u32[]{:S(2)}, u32[]{:S(2)}) collective-permute-start(bf16[2,512,128]{2,1,0:T(8,128)(2,1)S(1)} %collective-permute-done.11), channel_id=1, source_target_pairs={{0,192},{32,224},{64,0},{96,32},{128,64},{160,96},{192,128},{224,1... | collective-permute-start | bytes 786440 | tf_op jit(solution)/shard_map/ppermute | solution.py:55
  123.7 1.3 %copy-start = (bf16[2,4,2,512,128]{4,3,2,1,0:T(8,128)(2,1)}, bf16[2,4,2,512,128]{4,3,2,1,0:T(8,128)(2,1)S(1)}, u32[]{:S(2)}) copy-start(bf16[2,4,2,512,128]{4,3,2,1,0:T(8,128)(2,1)S(1)} %bitcast_dynamic-update-slice_fusion) | copy-start | bytes 6291460
